TPU v7x, 256 devices: a whole 4x4x8 slice. The times are simulated.
256 devices in a mesh: gx: 32 (over z_hi, x, core), gy: 4 (over y), gz: 2 (over z_lo).
Axes of the slice: x: 4, y: 4, z: 8 (z_hi: 4, z_lo: 2; z = z_hi * 2 + z_lo), core: 2. Of those that a mesh axis runs over, the one named last changes fastest.
Arguments:
- unary: bfloat16 [128, 32, 128, 128], P('gx', 'gy', 'gz'), may hold values from -3 to 3
- compat: float32 [6, 128, 128], replicated, may hold values from -2.5 to 2.5
- saved_first: bfloat16 [6, 128, 32, 128, 128], P(None, 'gx', 'gy', 'gz'), may hold values from 0.25 to 4
- saved_second: bfloat16 [6, 128, 32, 128, 128], P(None, 'gx', 'gy', 'gz'), may hold values from 0.25 to 4
- cotangent: float32 [128, 32, 128, 128], P('gx', 'gy', 'gz'), may hold values from -6 to 6
Outputs:
- grad_unary: float32 [128, 32, 128, 128], P('gx', 'gy', 'gz')
- grad_compat: float32 [6, 128, 128], replicated
All inputs are finite; a program needn't handle non-finite values.
Results may differ from a plain program's by a relative error of at most 0.0084.
Values may be sent and summed in bfloat16 or wider, within the bound.
No kernel may reach another device: no remote copies, remote signals or barrier semaphores. Data moves between devices by JAX's collectives and lax.ppermute only.
A program may use at most 128 MiB of HBM per device.

v0:
```python
import jax
import jax.numpy as jnp
from jax import lax
from jax.sharding import PartitionSpec as P

OPPOSE = (1, 0, 3, 2, 5, 4)


def extended(cells, sides, width):
    for axis, dim in sides:
        count = lax.axis_size(axis)
        ends = count - 1
        head = lax.slice_in_dim(cells, 0, width, axis=dim)
        tail = lax.slice_in_dim(cells, cells.shape[dim] - width, cells.shape[dim], axis=dim)
        cells = jnp.concatenate(
            [
                lax.ppermute(tail, axis, [(i, (i + 1) % count) for i in range(ends)]),
                cells,
                lax.ppermute(head, axis, [((i + 1) % count, i) for i in range(ends)]),
            ],
            axis=dim,
        )
    return cells


def full_product(fields):
    result = fields[0]
    for index in range(1, 6):
        result = result * fields[index]
    return result


def send_terms(potential, messages, whole, weights_b):
    labels = potential.shape[-1]
    scaled = potential * whole
    hidden = [scaled / messages[OPPOSE[direction]] for direction in range(6)]
    hidden_b = jnp.stack(hidden).astype(jnp.bfloat16)
    outgoing = jnp.einsum(
        "dxyzk,dkl->dxyzl", hidden_b, weights_b, preferred_element_type=jnp.float32
    )
    totals = jnp.sum(outgoing, axis=-1, keepdims=True)
    normal = labels * outgoing / totals
    return (hidden_b, normal, totals)


def trade(low_face, high_face, axis_dim):
    packed = jnp.concatenate([low_face, high_face], axis=axis_dim)
    if axis_dim == 0:
        rims = extended(packed, (("gx", 0),), 1)
    elif axis_dim == 1:
        rims = extended(packed, (("gy", 1),), 1)
    else:
        rims = extended(packed, (("gz", 2),), 1)
    lower = lax.slice_in_dim(rims, 0, 1, axis=axis_dim)
    upper = lax.slice_in_dim(rims, 3, 4, axis=axis_dim)
    return (lower, upper)


def spread(normal_b, lower_edge, upper_edge):
    result = []
    for axis_dim in range(3):
        plus = normal_b[2 * axis_dim]
        minus = normal_b[2 * axis_dim + 1]
        length = plus.shape[axis_dim]
        lower, upper = trade(
            lax.slice_in_dim(minus, 0, 1, axis=axis_dim),
            lax.slice_in_dim(plus, length - 1, length, axis=axis_dim),
            axis_dim,
        )
        ones = jnp.ones_like(lower)
        lower = jnp.where(lower_edge[axis_dim], ones, lower)
        upper = jnp.where(upper_edge[axis_dim], ones, upper)
        result.append(
            jnp.concatenate(
                [lower, lax.slice_in_dim(plus, 0, length - 1, axis=axis_dim)], axis=axis_dim
            )
        )
        result.append(
            jnp.concatenate(
                [lax.slice_in_dim(minus, 1, length, axis=axis_dim), upper], axis=axis_dim
            )
        )
    return result


def gather_back(grad_b):
    result = []
    for axis_dim in range(3):
        plus = grad_b[2 * axis_dim]
        minus = grad_b[2 * axis_dim + 1]
        length = plus.shape[axis_dim]
        lower, upper = trade(
            lax.slice_in_dim(plus, 0, 1, axis=axis_dim),
            lax.slice_in_dim(minus, length - 1, length, axis=axis_dim),
            axis_dim,
        )
        result.append(
            jnp.concatenate(
                [lax.slice_in_dim(plus, 1, length, axis=axis_dim), upper], axis=axis_dim
            )
        )
        result.append(
            jnp.concatenate(
                [lower, lax.slice_in_dim(minus, 0, length - 1, axis=axis_dim)], axis=axis_dim
            )
        )
    return jnp.stack(result).astype(jnp.float32)


def belief_adjoint(potential, arriving, cotangent):
    labels = potential.shape[-1]
    whole = full_product(arriving)
    joint = potential * whole
    summed = jnp.sum(joint, axis=-1, keepdims=True)
    belief = joint / summed
    grad_joint = labels * (cotangent - jnp.sum(cotangent * belief, axis=-1, keepdims=True)) / summed
    grad_potential = grad_joint * whole
    scaled = grad_joint * joint
    grad_arriving = [(scaled / arriving[edge]).astype(jnp.bfloat16) for edge in range(6)]
    return (grad_arriving, grad_potential)


def local_adjoint(grad_normal, normal, totals, hidden_b, weights_b):
    labels = normal.shape[-1]
    inner = jnp.sum(grad_normal * normal, axis=-1, keepdims=True)
    grad_out = (labels / totals * (grad_normal - inner / labels)).astype(jnp.bfloat16)
    grad_weights = jnp.einsum(
        "dxyzk,dxyzl->dkl", hidden_b, grad_out, preferred_element_type=jnp.float32
    )
    grad_hidden = jnp.einsum(
        "dxyzl,dkl->dxyzk", grad_out, weights_b, preferred_element_type=jnp.float32
    )
    return (grad_weights, grad_hidden)


def adjoint_terms(grad_hidden, potential, messages, whole):
    ratios = [grad_hidden[OPPOSE[index]] / messages[index] for index in range(6)]
    total = ratios[0]
    for index in range(1, 6):
        total = total + ratios[index]
    unary_term = whole * total
    scaled = potential * whole
    grad_messages = []
    for edge in range(6):
        partial_sum = None
        for index in range(6):
            if index == edge:
                continue
            partial_sum = ratios[index] if partial_sum is None else partial_sum + ratios[index]
        grad_messages.append((partial_sum * (scaled / messages[edge])).astype(jnp.bfloat16))
    return (unary_term, grad_messages)


def body(unary, compat, saved_first, saved_second, cotangent):
    potential = jnp.exp(unary.astype(jnp.float32))
    weights = jnp.exp(compat)
    weights_b = weights.astype(jnp.bfloat16)
    lower_edge = (lax.axis_index("gx") == 0, lax.axis_index("gy") == 0, lax.axis_index("gz") == 0)
    upper_edge = (
        lax.axis_index("gx") == lax.axis_size("gx") - 1,
        lax.axis_index("gy") == lax.axis_size("gy") - 1,
        lax.axis_index("gz") == lax.axis_size("gz") - 1,
    )
    first = [saved_first[index].astype(jnp.float32) for index in range(6)]
    second = [saved_second[index].astype(jnp.float32) for index in range(6)]
    whole_two = full_product(second)
    hidden_two, normal_two, totals_two = send_terms(potential, second, whole_two, weights_b)
    arriving = spread(
        [normal_two[index].astype(jnp.bfloat16) for index in range(6)], lower_edge, upper_edge
    )
    arriving = [value.astype(jnp.float32) for value in arriving]
    grad_arriving, grad_potential = belief_adjoint(potential, arriving, cotangent)
    grad_normal_two = gather_back(grad_arriving)
    weights_two, grad_hidden_two = local_adjoint(
        grad_normal_two, normal_two, totals_two, hidden_two, weights_b
    )
    unary_two, grad_second = adjoint_terms(grad_hidden_two, potential, second, whole_two)
    grad_potential = grad_potential + unary_two
    whole_one = full_product(first)
    hidden_one, normal_one, totals_one = send_terms(potential, first, whole_one, weights_b)
    grad_normal_one = gather_back(grad_second)
    weights_one, grad_hidden_one = local_adjoint(
        grad_normal_one, normal_one, totals_one, hidden_one, weights_b
    )
    ratios_one = [grad_hidden_one[OPPOSE[index]] / first[index] for index in range(6)]
    total_one = ratios_one[0]
    for index in range(1, 6):
        total_one = total_one + ratios_one[index]
    grad_potential = grad_potential + whole_one * total_one
    grad_unary = potential * grad_potential
    summed = lax.psum(weights_two + weights_one, ("gx", "gy", "gz"))
    grad_compat = weights * summed
    return (grad_unary, grad_compat)


def solution(mesh):
    placed = (
        P("gx", "gy", "gz", None),
        P(),
        P(None, "gx", "gy", "gz", None),
        P(None, "gx", "gy", "gz", None),
        P("gx", "gy", "gz", None),
    )
    return jax.shard_map(
        body,
        mesh=mesh,
        in_specs=placed,
        out_specs=(P("gx", "gy", "gz", None), P()),
        check_vma=False,
    )
```

profile of v0, /device:TPU:1, one launch (start us, length us, event | category | flops | bytes accessed | tf_op | source)
XLA Modules:
  0.0 413.3 jit_solution(10263491536333653765)
XLA Ops:
  7.2 4.7 %bitcast_dynamic-update-slice_fusion.5 = (bf16[6,4,8,64,128]{4,3,2,1,0:T(8,128)(2,1)S(1)}, f32[4,8,64,128]{3,2,1,0:T(8,128)S(1)}, bf16[6,4,8,64,128]{4,3,2,1,0:T(8,128)(2,1)S(1)}, f32[4,8,64,128]{3,2,1,0:T(8,128)S(1)}) fusion(bf16[6,4,8,64,128]{4,3,2,1,0:T(8,128)(2,1)} %param.7, bf16[4,8,64,128]{3,2,1,0:T(8,128)(2,1)} %param.5, ...), kind=kLoop, calls=%fused_computation.152 | loop fusion | flops 7602174 | bytes 9961472
  11.9 0.2 bitcast_dynamic-update-slice_fusion.10
  12.2 0.2 bitcast_dynamic-update-slice_fusion.9
  12.4 0.2 bitcast_dynamic-update-slice_fusion.8
  12.6 0.2 bitcast_dynamic-update-slice_fusion.7
  12.9 1.2 copy-done.3
  14.1 0.2 bitcast_dynamic-update-slice_fusion.4
  14.3 0.2 bitcast_dynamic-update-slice_fusion.3
  14.6 0.4 bitcast_dynamic-update-slice_fusion.2
  15.0 1.9 fusion.77
  17.0 2.0 fusion.13
  19.0 0.6 copy-done.2
  19.8 0.7 slice.293
  20.5 1.3 collective-permute-start.3
  21.7 0.6 slice.289
  22.4 5.3 %collective-permute-start.2 = (bf16[4,1,64,128]{3,2,1,0:T(8,128)(2,1)}, bf16[4,1,64,128]{3,2,1,0:T(8,128)(2,1)}, u32[]{:S(2)}, u32[]{:S(2)}) collective-permute-start(bf16[4,1,64,128]{3,2,1,0:T(8,128)(2,1)} %slice.289), channel_id=1, source_target_pairs={{0,2},{2,4},{4,6},{1,3},{3,5},{5,7},{8,10},{10,12},{12,14},{9,11},... | collective-permute-start | bytes 196616 | tf_op jit(solution)/shard_map/ppermute | solution.py:17
  27.6 0.6 slice.299
  28.2 1.3 collective-permute-start.5
  29.5 0.6 slice.295
  30.1 4.6 %collective-permute-start.4 = (bf16[4,8,1,128]{3,2,1,0:T(2,128)(2,1)}, bf16[4,8,1,128]{3,2,1,0:T(2,128)(2,1)S(1)}, u32[]{:S(2)}, u32[]{:S(2)}) collective-permute-start(bf16[4,8,1,128]{3,2,1,0:T(2,128)(2,1)} %slice.295), channel_id=1, source_target_pairs={{0,1},{2,3},{4,5},{6,7},{8,9},{10,11},{12,13},{14,15},{16,17},{18,... | collective-permute-start | bytes 24584 | tf_op jit(solution)/shard_map/ppermute | solution.py:17
  34.7 0.7 slice_bitcast_fusion.19
  35.4 5.6 %collective-permute-start.1 = (bf16[1,8,64,128]{3,2,1,0:T(8,128)(2,1)}, bf16[1,8,64,128]{3,2,1,0:T(8,128)(2,1)}, u32[]{:S(2)}, u32[]{:S(2)}) collective-permute-start(bf16[1,8,64,128]{3,2,1,0:T(8,128)(2,1)} %get-tuple-element.20), channel_id=1, source_target_pairs={{8,0},{16,8},{24,16},{32,24},{40,32},{48,40},{56,48},{64,56},{72,6... | collective-permute-start | bytes 393224 | tf_op jit(solution)/shard_map/ppermute | solution.py:19
  41.0 0.9 slice_bitcast_fusion.17
  41.9 0.2 bitcast_dynamic-update-slice_fusion.1
  42.1 0.2 bitcast_dynamic-update-slice_fusion
  42.4 4.4 %fusion.78 = (f32[6,4,8,64]{3,2,1,0:T(8,128)S(1)}, f32[6,4,8,64,128]{4,3,2,1,0:T(8,128)}) fusion(bf16[6,4,8,64,128]{4,3,2,1,0:T(8,128)(2,1)S(1)} %bitcast_dynamic-update-slice_fusion, bf16[6,128,128,1,1]{2,1,4,3,0:T(8,128)(2,1)S(1)} %fusion.68), kind=kOutput, calls=%fused_computation.182 | convolution fusion | flops 404213760 | bytes 9682944 | tf_op jit(solution)/shard_map/dxyzk,dkl->dxyzl/dot_general | solution.py:38
  46.8 0.6 broadcast_divide_fusion.1
  47.4 1.0 slice.298
  48.4 1.1 slice.292
  49.5 2.2 collective-permute-start
  51.8 0.8 broadcast_select_fusion.4
  52.6 0.9 broadcast_select_fusion.2
  53.5 0.9 broadcast_select_fusion
  54.4 2.0 fusion.72
  56.5 11.9 %fusion.37 = (bf16[4,8,64,128]{3,2,1,0:T(8,128)(2,1)S(1)}, f32[4,8,64,128]{3,2,1,0:T(8,128)S(1)}, f32[4,8,64,128]{3,2,1,0:T(8,128)}) fusion(bf16[4,8,1,128]{3,2,1,0:T(2,128)(2,1)S(1)} %broadcast_select_fusion.4, bf16[4,8,63,128]{3,2,1,0:T(8,128)(2,1)S(1)} %copy-done.14, f32[4,8,64,128]{3,2,1,0:T(8,128)S(1)} %get-tuple-element.13, ...), kind=kOutput, calls=%fused_computation.75 | output fusion | flops 4196479 | bytes 5775360 | tf_op jit(solution)/shard_map/sub | solution.py:116
  68.4 0.8 fusion.36
  69.3 2.5 collective-permute-start.6
  71.8 3.2 collective-permute-start.7
  75.4 1.4 collective-permute-start.8
  76.8 4.0 collective-permute-start.9
  80.8 1.3 collective-permute-start.10
  82.2 4.0 collective-permute-start.11
  86.6 0.4 collective-permute-done.11
  87.0 0.2 fusion.60
  87.3 3.8 fusion.1
  91.1 5.5 %fusion.79 = f32[6,4,8,64,128]{4,3,2,1,0:T(8,128)S(1)} fusion(bf16[6,128,128,1,1]{2,1,4,3,0:T(8,128)(2,1)S(1)} %fusion.68, bf16[6,4,8,64,128]{4,3,2,1,0:T(8,128)(2,1)S(1)} %fusion.60, f32[6,4,8,64]{3,2,1,0:T(8,128)S(1)} %broadcast_multiply_fusion.1, f32[6,4,8,64]{3,2,1,0:T(8,128)S(1)} %copy-done.18), kind=kOutput, calls=%fused_computation.183 | convolution fusion | flops 408944640 | bytes 9732096 | tf_op jit(solution)/shard_map/dxyzl,dkl->dxyzk/dot_general | solution.py:130
  96.6 1.1 multiply_convert_fusion
  97.7 0.5 multiply_convert_fusion.1
  98.2 1.0 multiply_convert_fusion.5
  99.2 1.2 multiply_convert_fusion.2
  100.4 4.2 %collective-permute-start.13 = (bf16[1,8,64,128]{3,2,1,0:T(8,128)(2,1)S(1)}, bf16[1,8,64,128]{3,2,1,0:T(8,128)(2,1)S(1)}, u32[]{:S(2)}, u32[]{:S(2)}) collective-permute-start(bf16[1,8,64,128]{3,2,1,0:T(8,128)(2,1)S(1)} %slice.320), channel_id=1, source_target_pairs={{0,8},{8,16},{16,24},{24,32},{32,40},{40,48},{48,56},{56,64},{64,7... | collective-permute-start | bytes 393224 | tf_op jit(solution)/shard_map/ppermute | solution.py:17
  104.7 2.2 collective-permute-start.12
  106.9 5.7 %fusion.17 = f32[6,128,128]{2,1,0:T(8,128)S(1)} fusion(bf16[6,4,8,64,128]{4,3,2,1,0:T(8,128)(2,1)S(1)} %copy-done.10, bf16[6,4,8,64,128]{4,3,2,1,0:T(8,128)(2,1)S(1)} %fusion.60, f32[6,4,8,64]{3,2,1,0:T(8,128)S(1)} %broadcast_multiply_fusion.1, f32[6,4,8,64]{3,2,1,0:T(8,128)S(1)} %copy-done.18), kind=kOutput, calls=%fused_computation.67 | convolution fusion | flops 408944640 | bytes 6782976 | tf_op jit(solution)/shard_map/dxyzk,dxyzl->dkl/dot_general | solution.py:127
  112.9 1.3 collective-permute-start.14
  114.2 4.0 collective-permute-start.15
  118.2 1.3 collective-permute-start.16
  119.5 4.2 %collective-permute-start.17 = (bf16[4,8,1,128]{3,2,1,0:T(2,128)(2,1)S(1)}, bf16[4,8,1,128]{3,2,1,0:T(2,128)(2,1)S(1)}, u32[]{:S(2)}, u32[]{:S(2)}) collective-permute-start(bf16[4,8,1,128]{3,2,1,0:T(2,128)(2,1)S(1)} %slice.328), channel_id=1, source_target_pairs={{0,1},{2,3},{4,5},{6,7},{8,9},{10,11},{12,13},{14,15},{16,17},{18,... | collective-permute-start | bytes 24584 | tf_op jit(solution)/shard_map/ppermute | solution.py:17
  124.4 0.2 fusion.66
  124.6 3.8 fusion.4
  128.5 6.8 %fusion.80 = f32[6,4,8,64,128]{4,3,2,1,0:T(8,128)} fusion(bf16[6,128,128,1,1]{2,1,4,3,0:T(8,128)(2,1)S(1)} %fusion.68, bf16[6,4,8,64,128]{4,3,2,1,0:T(8,128)(2,1)S(1)} %fusion.66, f32[6,4,8,64]{3,2,1,0:T(8,128)S(1)} %broadcast_multiply_fusion, f32[6,4,8,64]{3,2,1,0:T(8,128)S(1)} %broadcast_divide_fusion), kind=kOutput, calls=%fused_computation.184 | convolution fusion | flops 408944640 | bytes 9732096 | tf_op jit(solution)/shard_map/dxyzl,dkl->dxyzk/dot_general | solution.py:130
  135.3 6.2 %fusion.27 = f32[6,128,128]{2,1,0:T(8,128)} fusion(f32[6,128,128]{2,1,0:T(8,128)S(1)} %fusion.17, bf16[6,4,8,64,128]{4,3,2,1,0:T(8,128)(2,1)S(1)} %copy-done.8, bf16[6,4,8,64,128]{4,3,2,1,0:T(8,128)(2,1)S(1)} %fusion.66, f32[6,4,8,64]{3,2,1,0:T(8,128)S(1)} %broadcast_multiply_fusion, f32[6,4,8,64]{3,2,1,0:T(8,128)S(1)} %broadcast_divide_fusion), kind=kOutput, calls=%fused_computation.69 | convolution fusion | flops 409042944 | bytes 7176192 | tf_op jit(solution)/shard_map/dxyzk,dxyzl->dkl/dot_general | solution.py:127
  141.5 7.3 %fusion.46 = f32[4,8,64,128]{3,2,1,0:T(8,128)} fusion(f32[6,4,8,64,128]{4,3,2,1,0:T(8,128)} %fusion.80, f32[4,8,64,128]{3,2,1,0:T(8,128)S(1)} %get-tuple-element.9, f32[4,8,64,128]{3,2,1,0:T(8,128)} %get-tuple-element.36, f32[4,8,64,128]{3,2,1,0:T(8,128)} %copy-done.11, bf16[4,8,64,128]{3,2,1,0:T(8,128)(2,1)} %param.5, f32[4,8,64,128]{3,2,1,0:T(8,128)S(1)} %copy-done.5, ...), kind=kLoop, calls=%fused_computation.84 | loop fusion | flops 11010048 | bytes 19398656 | tf_op jit(solution)/shard_map/mul | solution.py:190
  148.9 255.7 %all-reduce.2.cloned.1.call-done = f32[6,128,128]{2,1,0:T(8,128)} async-done(((f32[6,128,128]{2,1,0:T(8,128)}), f32[6,128,128]{2,1,0:T(8,128)}) %all-reduce.2.cloned.1.call-update) | async-done | bytes 393232 | tf_op jit(solution)/shard_map/psum | solution.py:191
  404.5 1.9 exponential_multiply_fusion
  (109 shorter events, 2.2 us)
Async XLA Ops:
  7.2 397.4 %all-reduce.2.cloned.1.call-start = ((), (), s32[]{:S(2)}) async-start(), calls=%async_computation | async-start | bytes 786432 | tf_op jit(solution)/shard_map/psum | solution.py:191
  7.2 4.7 %copy-start = (bf16[6,4,8,64,128]{4,3,2,1,0:T(8,128)(2,1)S(1)}, bf16[6,4,8,64,128]{4,3,2,1,0:T(8,128)(2,1)}, u32[]{:S(2)}) copy-start(bf16[6,4,8,64,128]{4,3,2,1,0:T(8,128)(2,1)} %param.8) | copy-start | bytes 9437188
  12.2 1.9 copy-start.3
  12.6 1.9 copy-start.17
  15.0 1.9 copy-start.9
  16.9 2.7 copy-start.2
  19.8 22.6 %copy-start.16 = (bf16[4,8,64,128]{3,2,1,0:T(8,128)(2,1)}, bf16[4,8,64,128]{3,2,1,0:T(8,128)(2,1)S(1)}, u32[]{:S(2)}) copy-start(bf16[4,8,64,128]{3,2,1,0:T(8,128)(2,1)S(1)} %get-tuple-element.26) | copy-start | bytes 1572868
  20.5 32.1 %collective-permute-start.3 = (bf16[4,1,64,128]{3,2,1,0:T(8,128)(2,1)}, bf16[4,1,64,128]{3,2,1,0:T(8,128)(2,1)}, u32[]{:S(2)}, u32[]{:S(2)}) collective-permute-start(bf16[4,1,64,128]{3,2,1,0:T(8,128)(2,1)} %slice.293), channel_id=1, source_target_pairs={{2,0},{4,2},{6,4},{3,1},{5,3},{7,5},{10,8},{12,10},{14,12},{11,9},... | collective-permute-start | bytes 196616 | tf_op jit(solution)/shard_map/ppermute | solution.py:19
  22.4 31.1 %collective-permute-start.2 = (bf16[4,1,64,128]{3,2,1,0:T(8,128)(2,1)}, bf16[4,1,64,128]{3,2,1,0:T(8,128)(2,1)}, u32[]{:S(2)}, u32[]{:S(2)}) collective-permute-start(bf16[4,1,64,128]{3,2,1,0:T(8,128)(2,1)} %slice.289), channel_id=1, source_target_pairs={{0,2},{2,4},{4,6},{1,3},{3,5},{5,7},{8,10},{10,12},{12,14},{9,11},... | collective-permute-start | bytes 196616 | tf_op jit(solution)/shard_map/ppermute | solution.py:17
  28.2 21.3 %collective-permute-start.5 = (bf16[4,8,1,128]{3,2,1,0:T(2,128)(2,1)}, bf16[4,8,1,128]{3,2,1,0:T(2,128)(2,1)}, u32[]{:S(2)}, u32[]{:S(2)}) collective-permute-start(bf16[4,8,1,128]{3,2,1,0:T(2,128)(2,1)} %slice.299), channel_id=1, source_target_pairs={{1,0},{3,2},{5,4},{7,6},{9,8},{11,10},{13,12},{15,14},{17,16},{19,... | collective-permute-start | bytes 24584 | tf_op jit(solution)/shard_map/ppermute | solution.py:19
  30.1 22.4 %collective-permute-start.4 = (bf16[4,8,1,128]{3,2,1,0:T(2,128)(2,1)}, bf16[4,8,1,128]{3,2,1,0:T(2,128)(2,1)S(1)}, u32[]{:S(2)}, u32[]{:S(2)}) collective-permute-start(bf16[4,8,1,128]{3,2,1,0:T(2,128)(2,1)} %slice.295), channel_id=1, source_target_pairs={{0,1},{2,3},{4,5},{6,7},{8,9},{10,11},{12,13},{14,15},{16,17},{18,... | collective-permute-start | bytes 24584 | tf_op jit(solution)/shard_map/ppermute | solution.py:17
  35.4 18.0 %collective-permute-start.1 = (bf16[1,8,64,128]{3,2,1,0:T(8,128)(2,1)}, bf16[1,8,64,128]{3,2,1,0:T(8,128)(2,1)}, u32[]{:S(2)}, u32[]{:S(2)}) collective-permute-start(bf16[1,8,64,128]{3,2,1,0:T(8,128)(2,1)} %get-tuple-element.20), channel_id=1, source_target_pairs={{8,0},{16,8},{24,16},{32,24},{40,32},{48,40},{56,48},{64,56},{72,6... | collective-permute-start | bytes 393224 | tf_op jit(solution)/shard_map/ppermute | solution.py:19
  42.4 4.4 %copy-start.7 = (bf16[6,4,8,64,128]{4,3,2,1,0:T(8,128)(2,1)}, bf16[6,4,8,64,128]{4,3,2,1,0:T(8,128)(2,1)S(1)}, u32[]{:S(2)}) copy-start(bf16[6,4,8,64,128]{4,3,2,1,0:T(8,128)(2,1)S(1)} %bitcast_dynamic-update-slice_fusion) | copy-start | bytes 9437188
  46.8 7.7 %copy-start.6 = (bf16[4,8,64,128]{3,2,1,0:T(8,128)(2,1)S(1)}, bf16[4,8,64,128]{3,2,1,0:T(8,128)(2,1)}, u32[]{:S(2)}) copy-start(bf16[4,8,64,128]{3,2,1,0:T(8,128)(2,1)} %param.5) | copy-start | bytes 1572868
  49.5 7.0 %copy-start.14 = (bf16[4,8,63,128]{3,2,1,0:T(8,128)(2,1)S(1)}, bf16[4,8,63,128]{3,2,1,0:T(8,128)(2,1)}, u32[]{:S(2)}) copy-start(bf16[4,8,63,128]{3,2,1,0:T(8,128)(2,1)} %slice.298) | copy-start | bytes 1548292
  49.5 7.0 %copy-start.19 = (f32[4,8,64,128]{3,2,1,0:T(8,128)S(1)}, f32[4,8,64,128]{3,2,1,0:T(8,128)}, u32[]{:S(2)}) copy-start(f32[4,8,64,128]{3,2,1,0:T(8,128)} %param.9) | copy-start | bytes 3145732
  49.5 4.9 %collective-permute-start = (bf16[1,8,64,128]{3,2,1,0:T(8,128)(2,1)}, bf16[1,8,64,128]{3,2,1,0:T(8,128)(2,1)S(1)}, u32[]{:S(2)}, u32[]{:S(2)}) collective-permute-start(bf16[1,8,64,128]{3,2,1,0:T(8,128)(2,1)} %get-tuple-element.19), channel_id=1, source_target_pairs={{0,8},{8,16},{16,24},{24,32},{32,40},{40,48},{48,56},{56,64},{64,7... | collective-permute-start | bytes 393224 | tf_op jit(solution)/shard_map/ppermute | solution.py:17
  56.5 11.9 %copy-start.11 = (f32[4,8,64,128]{3,2,1,0:T(8,128)}, f32[4,8,64,128]{3,2,1,0:T(8,128)S(1)}, u32[]{:S(2)}) copy-start(f32[4,8,64,128]{3,2,1,0:T(8,128)S(1)} %get-tuple-element.13) | copy-start | bytes 3145732
  56.5 11.9 %copy-start.12 = (bf16[3,8,64,128]{3,2,1,0:T(8,128)(2,1)S(1)}, bf16[3,8,64,128]{3,2,1,0:T(8,128)(2,1)}, u32[]{:S(2)}) copy-start(bf16[3,8,64,128]{3,2,1,0:T(8,128)(2,1)} %get-tuple-element.21) | copy-start | bytes 1179652
  56.5 11.9 %copy-start.13 = (bf16[3,8,64,128]{3,2,1,0:T(8,128)(2,1)S(1)}, bf16[3,8,64,128]{3,2,1,0:T(8,128)(2,1)}, u32[]{:S(2)}) copy-start(bf16[3,8,64,128]{3,2,1,0:T(8,128)(2,1)} %get-tuple-element.22) | copy-start | bytes 1179652
  68.4 18.9 %slice-start = ((s8[6291456]{0:T(1024)(128)(4,1)}), s8[4194304]{0:T(1024)(128)(4,1)S(1)}, s32[]{:S(2)}) async-start(s8[6291456]{0:T(1024)(128)(4,1)} %bitcast.353), calls=%async_computation.1 | async-start | bytes 8388608
  69.3 12.9 %collective-permute-start.6 = (bf16[1,8,64,128]{3,2,1,0:T(8,128)(2,1)S(1)}, bf16[1,8,64,128]{3,2,1,0:T(8,128)(2,1)S(1)}, u32[]{:S(2)}, u32[]{:S(2)}) collective-permute-start(bf16[1,8,64,128]{3,2,1,0:T(8,128)(2,1)S(1)} %slice.301), channel_id=1, source_target_pairs={{8,0},{16,8},{24,16},{32,24},{40,32},{48,40},{56,48},{64,56},{72,6... | collective-permute-start | bytes 393224 | tf_op jit(solution)/shard_map/ppermute | solution.py:19
  71.8 14.4 %collective-permute-start.7 = (bf16[1,8,64,128]{3,2,1,0:T(8,128)(2,1)S(1)}, bf16[1,8,64,128]{3,2,1,0:T(8,128)(2,1)S(1)}, u32[]{:S(2)}, u32[]{:S(2)}) collective-permute-start(bf16[1,8,64,128]{3,2,1,0:T(8,128)(2,1)S(1)} %slice.302), channel_id=1, source_target_pairs={{0,8},{8,16},{16,24},{24,32},{32,40},{40,48},{48,56},{56,64},{64,7... | collective-permute-start | bytes 393224 | tf_op jit(solution)/shard_map/ppermute | solution.py:17
  75.1 12.2 %slice-start.1 = ((s8[6291456]{0:T(1024)(128)(4,1)}), s8[2097152]{0:T(1024)(128)(4,1)S(1)}, s32[]{:S(2)}) async-start(s8[6291456]{0:T(1024)(128)(4,1)} %bitcast.353), calls=%async_computation.2 | async-start | bytes 4194304
  75.4 10.9 %collective-permute-start.8 = (bf16[4,1,64,128]{3,2,1,0:T(8,128)(2,1)S(1)}, bf16[4,1,64,128]{3,2,1,0:T(8,128)(2,1)S(1)}, u32[]{:S(2)}, u32[]{:S(2)}) collective-permute-start(bf16[4,1,64,128]{3,2,1,0:T(8,128)(2,1)S(1)} %slice.305), channel_id=1, source_target_pairs={{2,0},{4,2},{6,4},{3,1},{5,3},{7,5},{10,8},{12,10},{14,12},{11,9},... | collective-permute-start | bytes 196616 | tf_op jit(solution)/shard_map/ppermute | solution.py:19
  76.8 9.6 %collective-permute-start.9 = (bf16[4,1,64,128]{3,2,1,0:T(8,128)(2,1)S(1)}, bf16[4,1,64,128]{3,2,1,0:T(8,128)(2,1)S(1)}, u32[]{:S(2)}, u32[]{:S(2)}) collective-permute-start(bf16[4,1,64,128]{3,2,1,0:T(8,128)(2,1)S(1)} %slice.306), channel_id=1, source_target_pairs={{0,2},{2,4},{4,6},{1,3},{3,5},{5,7},{8,10},{10,12},{12,14},{9,11},... | collective-permute-start | bytes 196616 | tf_op jit(solution)/shard_map/ppermute | solution.py:17
  80.8 5.6 %collective-permute-start.10 = (bf16[4,8,1,128]{3,2,1,0:T(2,128)(2,1)S(1)}, bf16[4,8,1,128]{3,2,1,0:T(2,128)(2,1)S(1)}, u32[]{:S(2)}, u32[]{:S(2)}) collective-permute-start(bf16[4,8,1,128]{3,2,1,0:T(2,128)(2,1)S(1)} %slice.309), channel_id=1, source_target_pairs={{1,0},{3,2},{5,4},{7,6},{9,8},{11,10},{13,12},{15,14},{17,16},{19,... | collective-permute-start | bytes 24584 | tf_op jit(solution)/shard_map/ppermute | solution.py:19
  82.2 4.8 %collective-permute-start.11 = (bf16[4,8,1,128]{3,2,1,0:T(2,128)(2,1)S(1)}, bf16[4,8,1,128]{3,2,1,0:T(2,128)(2,1)S(1)}, u32[]{:S(2)}, u32[]{:S(2)}) collective-permute-start(bf16[4,8,1,128]{3,2,1,0:T(2,128)(2,1)S(1)} %slice.310), channel_id=1, source_target_pairs={{0,1},{2,3},{4,5},{6,7},{8,9},{10,11},{12,13},{14,15},{16,17},{18,... | collective-permute-start | bytes 24584 | tf_op jit(solution)/shard_map/ppermute | solution.py:17
  87.3 3.8 copy-start.18
  91.1 5.5 %copy-start.1 = (bf16[6,4,8,64,128]{4,3,2,1,0:T(8,128)(2,1)S(1)}, bf16[6,4,8,64,128]{4,3,2,1,0:T(8,128)(2,1)}, u32[]{:S(2)}) copy-start(bf16[6,4,8,64,128]{4,3,2,1,0:T(8,128)(2,1)} %param.8) | copy-start | bytes 9437188
  97.7 1.4 copy-start.4
  99.2 13.4 %copy-start.15 = (bf16[4,8,64,128]{3,2,1,0:T(8,128)(2,1)}, bf16[4,8,64,128]{3,2,1,0:T(8,128)(2,1)S(1)}, u32[]{:S(2)}) copy-start(bf16[4,8,64,128]{3,2,1,0:T(8,128)(2,1)S(1)} %multiply_convert_fusion.5) | copy-start | bytes 1572868
  99.2 7.7 %copy-start.10 = (bf16[6,4,8,64,128]{4,3,2,1,0:T(8,128)(2,1)S(1)}, bf16[6,4,8,64,128]{4,3,2,1,0:T(8,128)(2,1)}, u32[]{:S(2)}) copy-start(bf16[6,4,8,64,128]{4,3,2,1,0:T(8,128)(2,1)} %copy-done.9) | copy-start | bytes 9437188
  99.2 25.4 %slice-start.2 = ((s8[6291456]{0:T(1024)(128)(4,1)}), s8[2097152]{0:T(1024)(128)(4,1)S(1)}, s32[]{:S(2)}) async-start(s8[6291456]{0:T(1024)(128)(4,1)} %bitcast.355), calls=%async_computation.3 | async-start | bytes 4194304
  100.4 23.4 %collective-permute-start.13 = (bf16[1,8,64,128]{3,2,1,0:T(8,128)(2,1)S(1)}, bf16[1,8,64,128]{3,2,1,0:T(8,128)(2,1)S(1)}, u32[]{:S(2)}, u32[]{:S(2)}) collective-permute-start(bf16[1,8,64,128]{3,2,1,0:T(8,128)(2,1)S(1)} %slice.320), channel_id=1, source_target_pairs={{0,8},{8,16},{16,24},{24,32},{32,40},{40,48},{48,56},{56,64},{64,7... | collective-permute-start | bytes 393224 | tf_op jit(solution)/shard_map/ppermute | solution.py:17
  104.7 20.0 %slice-start.3 = ((s8[6291456]{0:T(1024)(128)(4,1)}), s8[4194304]{0:T(1024)(128)(4,1)S(1)}, s32[]{:S(2)}) async-start(s8[6291456]{0:T(1024)(128)(4,1)} %bitcast.355), calls=%async_computation.4 | async-start | bytes 8388608
  104.7 14.9 %collective-permute-start.12 = (bf16[1,8,64,128]{3,2,1,0:T(8,128)(2,1)S(1)}, bf16[1,8,64,128]{3,2,1,0:T(8,128)(2,1)S(1)}, u32[]{:S(2)}, u32[]{:S(2)}) collective-permute-start(bf16[1,8,64,128]{3,2,1,0:T(8,128)(2,1)S(1)} %slice.319), channel_id=1, source_target_pairs={{8,0},{16,8},{24,16},{32,24},{40,32},{48,40},{56,48},{64,56},{72,6... | collective-permute-start | bytes 393224 | tf_op jit(solution)/shard_map/ppermute | solution.py:19
  112.6 11.2 %slice-start.4 = ((bf16[4,8,64,128]{3,2,1,0:T(8,128)(2,1)}), bf16[3,8,64,128]{3,2,1,0:T(8,128)(2,1)S(1)}, s32[]{:S(2)}) async-start(bf16[4,8,64,128]{3,2,1,0:T(8,128)(2,1)} %copy-done.15), calls=%async_computation.5 | async-start | bytes 786432 | tf_op jit(solution)/shard_map/slice | solution.py:99
  112.9 11.0 %collective-permute-start.14 = (bf16[4,1,64,128]{3,2,1,0:T(8,128)(2,1)S(1)}, bf16[4,1,64,128]{3,2,1,0:T(8,128)(2,1)S(1)}, u32[]{:S(2)}, u32[]{:S(2)}) collective-permute-start(bf16[4,1,64,128]{3,2,1,0:T(8,128)(2,1)S(1)} %slice.323), channel_id=1, source_target_pairs={{2,0},{4,2},{6,4},{3,1},{5,3},{7,5},{10,8},{12,10},{14,12},{11,9},... | collective-permute-start | bytes 196616 | tf_op jit(solution)/shard_map/ppermute | solution.py:19
  114.2 9.8 %collective-permute-start.15 = (bf16[4,1,64,128]{3,2,1,0:T(8,128)(2,1)S(1)}, bf16[4,1,64,128]{3,2,1,0:T(8,128)(2,1)S(1)}, u32[]{:S(2)}, u32[]{:S(2)}) collective-permute-start(bf16[4,1,64,128]{3,2,1,0:T(8,128)(2,1)S(1)} %slice.324), channel_id=1, source_target_pairs={{0,2},{2,4},{4,6},{1,3},{3,5},{5,7},{8,10},{10,12},{12,14},{9,11},... | collective-permute-start | bytes 196616 | tf_op jit(solution)/shard_map/ppermute | solution.py:17
  118.2 5.9 %collective-permute-start.16 = (bf16[4,8,1,128]{3,2,1,0:T(2,128)(2,1)S(1)}, bf16[4,8,1,128]{3,2,1,0:T(2,128)(2,1)S(1)}, u32[]{:S(2)}, u32[]{:S(2)}) collective-permute-start(bf16[4,8,1,128]{3,2,1,0:T(2,128)(2,1)S(1)} %slice.327), channel_id=1, source_target_pairs={{1,0},{3,2},{5,4},{7,6},{9,8},{11,10},{13,12},{15,14},{17,16},{19,... | collective-permute-start | bytes 24584 | tf_op jit(solution)/shard_map/ppermute | solution.py:19
  119.5 4.8 %collective-permute-start.17 = (bf16[4,8,1,128]{3,2,1,0:T(2,128)(2,1)S(1)}, bf16[4,8,1,128]{3,2,1,0:T(2,128)(2,1)S(1)}, u32[]{:S(2)}, u32[]{:S(2)}) collective-permute-start(bf16[4,8,1,128]{3,2,1,0:T(2,128)(2,1)S(1)} %slice.328), channel_id=1, source_target_pairs={{0,1},{2,3},{4,5},{6,7},{8,9},{10,11},{12,13},{14,15},{16,17},{18,... | collective-permute-start | bytes 24584 | tf_op jit(solution)/shard_map/ppermute | solution.py:17
  128.5 6.8 %copy-start.8 = (bf16[6,4,8,64,128]{4,3,2,1,0:T(8,128)(2,1)S(1)}, bf16[6,4,8,64,128]{4,3,2,1,0:T(8,128)(2,1)}, u32[]{:S(2)}) copy-start(bf16[6,4,8,64,128]{4,3,2,1,0:T(8,128)(2,1)} %copy-done.7) | copy-start | bytes 9437188
  135.3 6.3 %copy-start.5 = (f32[4,8,64,128]{3,2,1,0:T(8,128)S(1)}, f32[4,8,64,128]{3,2,1,0:T(8,128)}, u32[]{:S(2)}) copy-start(f32[4,8,64,128]{3,2,1,0:T(8,128)} %copy-done.4) | copy-start | bytes 3145732
Sparse Core Ops, SparseCore 0:
  141.7 262.8 all-reduce.1
where the time goes:
time: 414 us; the launch traced here: 413 us
  waiting for transfers between devices  256 us (62%)
  starting transfers between devices  53.8 us (13%)
  other arithmetic  48.6 us (12%)
  matrix products  30.4 us (7%)
  between operations  15.1 us (4%)
  local copies, waits for them, and re-layouts  9.02 us (2%)
    psum x1, waiting for transfers between devices, body(): summed = lax.psum(weights_two + weights_one, ('gx', 'gy', 'gz'))  256 us
    ppermute x9, starting transfers between devices, extended(): lax.ppermute(tail, axis, [(i, (i + 1) % count) for i in range(ends)])  35.6 us
    ppermute x9, starting transfers between devices, extended(): lax.ppermute(head, axis, [((i + 1) % count, i) for i in range(ends)])  18.1 us
    dot_general x2, matrix products, local_adjoint(): jnp.einsum('dxyzl,dkl->dxyzk', grad_out, weights_b, preferred_element_typ...  12.3 us
    dot_general x2, matrix products, local_adjoint(): jnp.einsum('dxyzk,dxyzl->dkl', hidden_b, grad_out, preferred_element_type...  11.9 us
    sub x1, other arithmetic, belief_adjoint(): cotangent - jnp.sum(cotangent * belief, axis=-1, keepdims=True)  11.9 us
  transfers between devices with their start and end apart: 19, of which 3 were waited for; matrix products, arithmetic and copies ran while one was open for 7% of the time, Pallas kernels for 0%

commit v1 on v0

--- a/solution.py
+++ b/solution.py
@@ -151,6 +151,16 @@
     return (unary_term, grad_messages)
 
 
+def all_sum(value, axes):
+    count = 1
+    for axis in axes:
+        count *= lax.axis_size(axis)
+    rows = value.reshape(count, -1)
+    mine = jnp.sum(lax.all_to_all(rows, axes, 0, 0, tiled=True), axis=0, keepdims=True)
+    spread_out = jnp.broadcast_to(mine, rows.shape)
+    return lax.all_to_all(spread_out, axes, 0, 0, tiled=True).reshape(value.shape)
+
+
 def body(unary, compat, saved_first, saved_second, cotangent):
     potential = jnp.exp(unary.astype(jnp.float32))
     weights = jnp.exp(compat)
@@ -188,7 +198,7 @@
         total_one = total_one + ratios_one[index]
     grad_potential = grad_potential + whole_one * total_one
     grad_unary = potential * grad_potential
-    summed = lax.psum(weights_two + weights_one, ("gx", "gy", "gz"))
+    summed = all_sum(weights_two + weights_one, ("gx", "gy", "gz"))
     grad_compat = weights * summed
     return (grad_unary, grad_compat)
 

time: 414 us -> 204 us (0.49)
  waiting for transfers between devices: 256 us -> 21.3 us
  starting transfers between devices: 53.8 us -> 84.8 us
  between operations: 15.1 us -> 1.78 us
    psum x1 -> x0, waiting for transfers between devices: 256 us -> none  [body(): summed = lax.psum(weights_two + weights_one, ('gx', 'gy', 'gz'))]
    all_to_all x0 -> x2, starting transfers between devices: none -> 31.2 us  [the longest x1 24 us: all_sum(): lax.all_to_all(rows, axes, 0, 0, tiled=True)]
    all_to_all x0 -> x2, waiting for transfers between devices: none -> 20.5 us  [the longest x1 10.3 us: all_sum(): lax.all_to_all(spread_out, axes, 0, 0, tiled=True).reshape(value.shape)]
  transfers between devices with their start and end apart: 19 -> 20, of which waited for: 3 -> 4; matrix products, arithmetic and copies ran while one was open for 7% -> 18% of each run, Pallas kernels for 0% -> 0%
where the time goes in v1:
time: 204 us; the launch traced here: 203 us
  starting transfers between devices  84.8 us (42%)
  other arithmetic  52.5 us (26%)
  matrix products  31 us (15%)
  waiting for transfers between devices  21.3 us (10%)
  local copies, waits for them, and re-layouts  11.7 us (6%)
    ppermute x9, starting transfers between devices, extended(): lax.ppermute(tail, axis, [(i, (i + 1) % count) for i in range(ends)])  35.2 us
    all_to_all x1, starting transfers between devices, all_sum(): lax.all_to_all(rows, axes, 0, 0, tiled=True)  24 us
    ppermute x9, starting transfers between devices, extended(): lax.ppermute(head, axis, [((i + 1) % count, i) for i in range(ends)])  18.4 us
    sub x1, other arithmetic, belief_adjoint(): cotangent - jnp.sum(cotangent * belief, axis=-1, keepdims=True)  14.3 us
    dot_general x2, matrix products, local_adjoint(): jnp.einsum('dxyzl,dkl->dxyzk', grad_out, weights_b, preferred_element_typ...  12.9 us
    dot_general x2, matrix products, local_adjoint(): jnp.einsum('dxyzk,dxyzl->dkl', hidden_b, grad_out, preferred_element_type...  11.9 us
    all_to_all x1, waiting for transfers between devices, all_sum(): lax.all_to_all(spread_out, axes, 0, 0, tiled=True).reshape(value.shape)  10.3 us
    all_to_all x1, waiting for transfers between devices, all_sum(): lax.all_to_all(rows, axes, 0, 0, tiled=True)  10.2 us
  transfers between devices with their start and end apart: 20, of which 4 were waited for; matrix products, arithmetic and copies ran while one was open for 18% of the time, Pallas kernels for 0%

profile of v1, /device:TPU:1, one launch (start us, length us, event | category | flops | bytes accessed | tf_op | source)
XLA Modules:
  0.0 203.2 jit_solution(8915856318108931900)
XLA Ops:
  0.6 4.7 %bitcast_dynamic-update-slice_fusion.5 = (bf16[6,4,8,64,128]{4,3,2,1,0:T(8,128)(2,1)S(1)}, f32[4,8,64,128]{3,2,1,0:T(8,128)S(1)}, bf16[6,4,8,64,128]{4,3,2,1,0:T(8,128)(2,1)S(1)}, f32[4,8,64,128]{3,2,1,0:T(8,128)S(1)}) fusion(bf16[6,4,8,64,128]{4,3,2,1,0:T(8,128)(2,1)} %param.7, bf16[4,8,64,128]{3,2,1,0:T(8,128)(2,1)} %param.5, ...), kind=kLoop, calls=%fused_computation.152 | loop fusion | flops 7602174 | bytes 9961472
  6.1 0.2 bitcast_dynamic-update-slice_fusion.7
  6.3 1.2 copy-done.4
  8.0 0.4 bitcast_dynamic-update-slice_fusion.2
  8.5 1.9 fusion.77
  10.4 2.0 fusion.13
  12.4 0.6 copy-done.3
  13.2 0.7 slice.293
  13.9 1.3 collective-permute-start.3
  15.1 0.6 slice.289
  15.8 5.3 %collective-permute-start.2 = (bf16[4,1,64,128]{3,2,1,0:T(8,128)(2,1)}, bf16[4,1,64,128]{3,2,1,0:T(8,128)(2,1)}, u32[]{:S(2)}, u32[]{:S(2)}) collective-permute-start(bf16[4,1,64,128]{3,2,1,0:T(8,128)(2,1)} %slice.289), channel_id=1, source_target_pairs={{0,2},{2,4},{4,6},{1,3},{3,5},{5,7},{8,10},{10,12},{12,14},{9,11},... | collective-permute-start | bytes 196616 | tf_op jit(solution)/shard_map/ppermute | solution.py:17
  21.0 0.6 slice.299
  21.6 1.3 collective-permute-start.5
  22.9 0.6 slice.295
  23.6 4.6 %collective-permute-start.4 = (bf16[4,8,1,128]{3,2,1,0:T(2,128)(2,1)}, bf16[4,8,1,128]{3,2,1,0:T(2,128)(2,1)S(1)}, u32[]{:S(2)}, u32[]{:S(2)}) collective-permute-start(bf16[4,8,1,128]{3,2,1,0:T(2,128)(2,1)} %slice.295), channel_id=1, source_target_pairs={{0,1},{2,3},{4,5},{6,7},{8,9},{10,11},{12,13},{14,15},{16,17},{18,... | collective-permute-start | bytes 24584 | tf_op jit(solution)/shard_map/ppermute | solution.py:17
  28.1 0.7 slice_bitcast_fusion.19
  28.8 5.6 %collective-permute-start.1 = (bf16[1,8,64,128]{3,2,1,0:T(8,128)(2,1)}, bf16[1,8,64,128]{3,2,1,0:T(8,128)(2,1)}, u32[]{:S(2)}, u32[]{:S(2)}) collective-permute-start(bf16[1,8,64,128]{3,2,1,0:T(8,128)(2,1)} %get-tuple-element.20), channel_id=1, source_target_pairs={{8,0},{16,8},{24,16},{32,24},{40,32},{48,40},{56,48},{64,56},{72,6... | collective-permute-start | bytes 393224 | tf_op jit(solution)/shard_map/ppermute | solution.py:19
  34.4 0.9 slice_bitcast_fusion.17
  35.8 4.3 %fusion.78 = (f32[6,4,8,64]{3,2,1,0:T(8,128)S(1)}, f32[6,4,8,64,128]{4,3,2,1,0:T(8,128)}) fusion(bf16[6,4,8,64,128]{4,3,2,1,0:T(8,128)(2,1)S(1)} %bitcast_dynamic-update-slice_fusion, bf16[6,128,128,1,1]{2,1,4,3,0:T(8,128)(2,1)S(1)} %fusion.68), kind=kOutput, calls=%fused_computation.182 | convolution fusion | flops 404213760 | bytes 9682944 | tf_op jit(solution)/shard_map/dxyzk,dkl->dxyzl/dot_general | solution.py:38
  40.1 0.6 broadcast_divide_fusion.1
  40.8 1.0 slice.298
  41.7 1.8 slice.290
  43.6 0.8 slice.292
  44.4 2.1 %collective-permute-start = (bf16[1,8,64,128]{3,2,1,0:T(8,128)(2,1)}, bf16[1,8,64,128]{3,2,1,0:T(8,128)(2,1)S(1)}, u32[]{:S(2)}, u32[]{:S(2)}) collective-permute-start(bf16[1,8,64,128]{3,2,1,0:T(8,128)(2,1)} %get-tuple-element.19), channel_id=1, source_target_pairs={{0,8},{8,16},{16,24},{24,32},{32,40},{40,48},{48,56},{56,64},{64,7... | collective-permute-start | bytes 393224 | tf_op jit(solution)/shard_map/ppermute | solution.py:17
  46.5 0.8 broadcast_select_fusion.4
  47.3 0.9 broadcast_select_fusion.2
  48.2 0.9 broadcast_select_fusion
  49.2 2.3 %fusion.72 = (f32[4,8,64]{2,1,0:T(8,128)S(1)}, f32[4,8,64,128]{3,2,1,0:T(8,128)S(1)}) fusion(bf16[4,8,64,128]{3,2,1,0:T(8,128)(2,1)S(1)} %copy-done.9, bf16[4,8,1,128]{3,2,1,0:T(2,128)(2,1)S(1)} %broadcast_select_fusion.4, bf16[4,8,63,128]{3,2,1,0:T(8,128)(2,1)} %slice.298, bf16[4,8,63,128]{3,2,1,0:T(8,128)(2,1)S(1)} %bitcast.359, ...), kind=kLoop, calls=%fused_computation.180 | loop fusion | flops 8386560 | bytes 4726784 | tf_op jit(solution)/shard_map/reduce_sum | solution.py:114
  51.5 14.3 %fusion.37 = (bf16[4,8,64,128]{3,2,1,0:T(8,128)(2,1)S(1)}, f32[4,8,64,128]{3,2,1,0:T(8,128)S(1)}, f32[4,8,64,128]{3,2,1,0:T(8,128)}) fusion(bf16[4,8,1,128]{3,2,1,0:T(2,128)(2,1)S(1)} %broadcast_select_fusion.4, bf16[4,8,63,128]{3,2,1,0:T(8,128)(2,1)} %slice.298, f32[4,8,64,128]{3,2,1,0:T(8,128)S(1)} %get-tuple-element.13, ...), kind=kOutput, calls=%fused_computation.75 | output fusion | flops 4196479 | bytes 5775360 | tf_op jit(solution)/shard_map/sub | solution.py:116
  65.9 0.8 fusion.36
  66.7 2.5 %collective-permute-start.6 = (bf16[1,8,64,128]{3,2,1,0:T(8,128)(2,1)S(1)}, bf16[1,8,64,128]{3,2,1,0:T(8,128)(2,1)S(1)}, u32[]{:S(2)}, u32[]{:S(2)}) collective-permute-start(bf16[1,8,64,128]{3,2,1,0:T(8,128)(2,1)S(1)} %slice.301), channel_id=1, source_target_pairs={{8,0},{16,8},{24,16},{32,24},{40,32},{48,40},{56,48},{64,56},{72,6... | collective-permute-start | bytes 393224 | tf_op jit(solution)/shard_map/ppermute | solution.py:19
  69.3 3.2 %collective-permute-start.7 = (bf16[1,8,64,128]{3,2,1,0:T(8,128)(2,1)S(1)}, bf16[1,8,64,128]{3,2,1,0:T(8,128)(2,1)S(1)}, u32[]{:S(2)}, u32[]{:S(2)}) collective-permute-start(bf16[1,8,64,128]{3,2,1,0:T(8,128)(2,1)S(1)} %slice.302), channel_id=1, source_target_pairs={{0,8},{8,16},{16,24},{24,32},{32,40},{40,48},{48,56},{56,64},{64,7... | collective-permute-start | bytes 393224 | tf_op jit(solution)/shard_map/ppermute | solution.py:17
  72.9 1.4 collective-permute-start.8
  74.3 4.0 %collective-permute-start.9 = (bf16[4,1,64,128]{3,2,1,0:T(8,128)(2,1)S(1)}, bf16[4,1,64,128]{3,2,1,0:T(8,128)(2,1)S(1)}, u32[]{:S(2)}, u32[]{:S(2)}) collective-permute-start(bf16[4,1,64,128]{3,2,1,0:T(8,128)(2,1)S(1)} %slice.306), channel_id=1, source_target_pairs={{0,2},{2,4},{4,6},{1,3},{3,5},{5,7},{8,10},{10,12},{12,14},{9,11},... | collective-permute-start | bytes 196616 | tf_op jit(solution)/shard_map/ppermute | solution.py:17
  78.3 1.3 collective-permute-start.10
  79.6 4.0 %collective-permute-start.11 = (bf16[4,8,1,128]{3,2,1,0:T(2,128)(2,1)S(1)}, bf16[4,8,1,128]{3,2,1,0:T(2,128)(2,1)S(1)}, u32[]{:S(2)}, u32[]{:S(2)}) collective-permute-start(bf16[4,8,1,128]{3,2,1,0:T(2,128)(2,1)S(1)} %slice.310), channel_id=1, source_target_pairs={{0,1},{2,3},{4,5},{6,7},{8,9},{10,11},{12,13},{14,15},{16,17},{18,... | collective-permute-start | bytes 24584 | tf_op jit(solution)/shard_map/ppermute | solution.py:17
  84.1 0.4 collective-permute-done.11
  84.5 0.2 fusion.60
  84.8 3.8 %fusion.1 = f32[6,4,8,64]{3,2,1,0:T(8,128)S(1)} fusion(bf16[6,4,8,64,128]{4,3,2,1,0:T(8,128)(2,1)S(1)} %fusion.60, f32[6,4,8,64]{3,2,1,0:T(8,128)S(1)} %get-tuple-element.34, f32[6,4,8,64,128]{4,3,2,1,0:T(8,128)S(1)} %bitcast.356), kind=kLoop, calls=%fused_computation.5 | loop fusion | flops 7852032 | bytes 9535488 | tf_op jit(solution)/shard_map/reduce_sum | solution.py:125
  88.6 5.5 %fusion.79 = f32[6,4,8,64,128]{4,3,2,1,0:T(8,128)S(1)} fusion(bf16[6,128,128,1,1]{2,1,4,3,0:T(8,128)(2,1)S(1)} %fusion.68, bf16[6,4,8,64,128]{4,3,2,1,0:T(8,128)(2,1)S(1)} %fusion.60, f32[6,4,8,64]{3,2,1,0:T(8,128)S(1)} %broadcast_multiply_fusion.1, f32[6,4,8,64]{3,2,1,0:T(8,128)S(1)} %copy-done.23), kind=kOutput, calls=%fused_computation.183 | convolution fusion | flops 408944640 | bytes 9732096 | tf_op jit(solution)/shard_map/dxyzl,dkl->dxyzk/dot_general | solution.py:130
  94.1 1.1 multiply_convert_fusion
  95.2 0.5 multiply_convert_fusion.1
  95.7 1.0 multiply_convert_fusion.5
  96.9 1.2 multiply_convert_fusion.2
  98.1 4.2 %collective-permute-start.13 = (bf16[1,8,64,128]{3,2,1,0:T(8,128)(2,1)S(1)}, bf16[1,8,64,128]{3,2,1,0:T(8,128)(2,1)S(1)}, u32[]{:S(2)}, u32[]{:S(2)}) collective-permute-start(bf16[1,8,64,128]{3,2,1,0:T(8,128)(2,1)S(1)} %slice.320), channel_id=1, source_target_pairs={{0,8},{8,16},{16,24},{24,32},{32,40},{40,48},{48,56},{56,64},{64,7... | collective-permute-start | bytes 393224 | tf_op jit(solution)/shard_map/ppermute | solution.py:17
  102.4 2.4 %collective-permute-start.12 = (bf16[1,8,64,128]{3,2,1,0:T(8,128)(2,1)S(1)}, bf16[1,8,64,128]{3,2,1,0:T(8,128)(2,1)S(1)}, u32[]{:S(2)}, u32[]{:S(2)}) collective-permute-start(bf16[1,8,64,128]{3,2,1,0:T(8,128)(2,1)S(1)} %slice.319), channel_id=1, source_target_pairs={{8,0},{16,8},{24,16},{32,24},{40,32},{48,40},{56,48},{64,56},{72,6... | collective-permute-start | bytes 393224 | tf_op jit(solution)/shard_map/ppermute | solution.py:19
  104.8 5.7 %fusion.17 = f32[6,128,128]{2,1,0:T(8,128)S(1)} fusion(bf16[6,4,8,64,128]{4,3,2,1,0:T(8,128)(2,1)S(1)} %copy-done.13, bf16[6,4,8,64,128]{4,3,2,1,0:T(8,128)(2,1)S(1)} %fusion.60, f32[6,4,8,64]{3,2,1,0:T(8,128)S(1)} %broadcast_multiply_fusion.1, f32[6,4,8,64]{3,2,1,0:T(8,128)S(1)} %copy-done.23), kind=kOutput, calls=%fused_computation.67 | convolution fusion | flops 408944640 | bytes 6782976 | tf_op jit(solution)/shard_map/dxyzk,dxyzl->dkl/dot_general | solution.py:127
  110.8 1.3 collective-permute-start.14
  112.1 4.0 %collective-permute-start.15 = (bf16[4,1,64,128]{3,2,1,0:T(8,128)(2,1)S(1)}, bf16[4,1,64,128]{3,2,1,0:T(8,128)(2,1)S(1)}, u32[]{:S(2)}, u32[]{:S(2)}) collective-permute-start(bf16[4,1,64,128]{3,2,1,0:T(8,128)(2,1)S(1)} %slice.324), channel_id=1, source_target_pairs={{0,2},{2,4},{4,6},{1,3},{3,5},{5,7},{8,10},{10,12},{12,14},{9,11},... | collective-permute-start | bytes 196616 | tf_op jit(solution)/shard_map/ppermute | solution.py:17
  116.1 1.3 collective-permute-start.16
  117.4 4.0 %collective-permute-start.17 = (bf16[4,8,1,128]{3,2,1,0:T(2,128)(2,1)S(1)}, bf16[4,8,1,128]{3,2,1,0:T(2,128)(2,1)S(1)}, u32[]{:S(2)}, u32[]{:S(2)}) collective-permute-start(bf16[4,8,1,128]{3,2,1,0:T(2,128)(2,1)S(1)} %slice.328), channel_id=1, source_target_pairs={{0,1},{2,3},{4,5},{6,7},{8,9},{10,11},{12,13},{14,15},{16,17},{18,... | collective-permute-start | bytes 24584 | tf_op jit(solution)/shard_map/ppermute | solution.py:17
  121.9 0.4 collective-permute-done.17
  122.3 0.2 fusion.66
  122.6 3.8 %fusion.4 = f32[6,4,8,64]{3,2,1,0:T(8,128)S(1)} fusion(bf16[6,4,8,64,128]{4,3,2,1,0:T(8,128)(2,1)S(1)} %fusion.66, f32[6,4,8,64,128]{4,3,2,1,0:T(8,128)S(1)} %bitcast.358, f32[6,4,8,64]{3,2,1,0:T(8,128)S(1)} %get-tuple-element.37), kind=kLoop, calls=%fused_computation.8 | loop fusion | flops 7852032 | bytes 9535488 | tf_op jit(solution)/shard_map/reduce_sum | solution.py:125
  126.4 6.3 %fusion.27 = f32[6,128,128]{2,1,0:T(8,128)} fusion(f32[6,128,128]{2,1,0:T(8,128)S(1)} %fusion.17, bf16[6,4,8,64,128]{4,3,2,1,0:T(8,128)(2,1)S(1)} %copy-done.11, bf16[6,4,8,64,128]{4,3,2,1,0:T(8,128)(2,1)S(1)} %fusion.66, f32[6,4,8,64]{3,2,1,0:T(8,128)S(1)} %broadcast_multiply_fusion, f32[6,4,8,64]{3,2,1,0:T(8,128)S(1)} %broadcast_divide_fusion), kind=kOutput, calls=%fused_computation.69 | convolution fusion | flops 409042944 | bytes 7176192 | tf_op jit(solution)/shard_map/dxyzk,dxyzl->dkl/dot_general | solution.py:127
  132.7 24.0 %all-to-all-start = ((f32[256,1,384]{2,1,0:T(1,128)}), f32[256,1,384]{2,1,0:T(1,128)}, u32[]{:S(2)}, u32[]{:S(2)}) async-start(f32[256,1,384]{2,1,0:T(1,128)} %bitcast.75), calls=%async_computation | async-start | bytes 786432 | tf_op jit(solution)/shard_map/all_to_all | solution.py:159
  156.8 7.3 %fusion.80 = f32[6,4,8,64,128]{4,3,2,1,0:T(8,128)} fusion(bf16[6,128,128,1,1]{2,1,4,3,0:T(8,128)(2,1)S(1)} %fusion.68, bf16[6,4,8,64,128]{4,3,2,1,0:T(8,128)(2,1)} %copy-done.7, f32[6,4,8,64]{3,2,1,0:T(8,128)S(1)} %broadcast_multiply_fusion, f32[6,4,8,64]{3,2,1,0:T(8,128)} %copy-done.24), kind=kOutput, calls=%fused_computation.184 | convolution fusion | flops 408944640 | bytes 9732096 | tf_op jit(solution)/shard_map/dxyzl,dkl->dxyzk/dot_general | solution.py:130
  164.1 10.2 %all-to-all-done = f32[256,1,384]{2,1,0:T(1,128)} async-done(((f32[256,1,384]{2,1,0:T(1,128)}), f32[256,1,384]{2,1,0:T(1,128)}, u32[]{:S(2)}, u32[]{:S(2)}) %all-to-all-start) | async-done | bytes 393248 | tf_op jit(solution)/shard_map/all_to_all | solution.py:159
  174.3 1.3 reduce_sum.69
  175.6 1.0 broadcast_in_dim.11
  176.5 7.2 %all-to-all-start.1 = ((f32[256,1,384]{2,1,0:T(1,128)}), f32[256,1,384]{2,1,0:T(1,128)}, u32[]{:S(2)}, u32[]{:S(2)}) async-start(f32[256,1,384]{2,1,0:T(1,128)} %broadcast_in_dim.11), calls=%async_computation.1 | async-start | bytes 786432 | tf_op jit(solution)/shard_map/all_to_all | solution.py:161
  183.8 7.4 %fusion.46 = f32[4,8,64,128]{3,2,1,0:T(8,128)} fusion(f32[6,4,8,64,128]{4,3,2,1,0:T(8,128)} %fusion.80, f32[4,8,64,128]{3,2,1,0:T(8,128)} %copy-done.6, f32[4,8,64,128]{3,2,1,0:T(8,128)} %get-tuple-element.36, f32[4,8,64,128]{3,2,1,0:T(8,128)} %copy-done.14, bf16[4,8,64,128]{3,2,1,0:T(8,128)(2,1)} %param.5, f32[4,8,64,128]{3,2,1,0:T(8,128)} %copy-done.8, ...), kind=kLoop, calls=%fused_computation.84 | loop fusion | flops 11010048 | bytes 19398656 | tf_op jit(solution)/shard_map/mul | solution.py:200
  191.1 10.3 %all-to-all-done.1 = f32[256,1,384]{2,1,0:T(1,128)} async-done(((f32[256,1,384]{2,1,0:T(1,128)}), f32[256,1,384]{2,1,0:T(1,128)}, u32[]{:S(2)}, u32[]{:S(2)}) %all-to-all-start.1) | async-done | bytes 393248 | tf_op jit(solution)/shard_map/all_to_all | solution.py:161
  201.4 1.8 exponential_multiply_fusion
  (122 shorter events, 3.6 us)
Async XLA Ops:
  0.6 4.7 %copy-start = (bf16[6,4,8,64,128]{4,3,2,1,0:T(8,128)(2,1)S(1)}, bf16[6,4,8,64,128]{4,3,2,1,0:T(8,128)(2,1)}, u32[]{:S(2)}) copy-start(bf16[6,4,8,64,128]{4,3,2,1,0:T(8,128)(2,1)} %param.8) | copy-start | bytes 9437188
  5.6 1.9 copy-start.4
  6.0 1.9 copy-start.21
  8.5 1.9 copy-start.12
  10.4 2.6 %copy-start.3 = (f32[6,4,8,64,128]{4,3,2,1,0:T(8,128)}, f32[6,4,8,64,128]{4,3,2,1,0:T(8,128)S(1)}, u32[]{:S(2)}) copy-start(f32[6,4,8,64,128]{4,3,2,1,0:T(8,128)S(1)} %get-tuple-element.35) | copy-start | bytes 18874372
  13.2 22.6 %copy-start.20 = (bf16[4,8,64,128]{3,2,1,0:T(8,128)(2,1)}, bf16[4,8,64,128]{3,2,1,0:T(8,128)(2,1)S(1)}, u32[]{:S(2)}) copy-start(bf16[4,8,64,128]{3,2,1,0:T(8,128)(2,1)S(1)} %get-tuple-element.23) | copy-start | bytes 1572868
  13.9 33.4 %collective-permute-start.3 = (bf16[4,1,64,128]{3,2,1,0:T(8,128)(2,1)}, bf16[4,1,64,128]{3,2,1,0:T(8,128)(2,1)}, u32[]{:S(2)}, u32[]{:S(2)}) collective-permute-start(bf16[4,1,64,128]{3,2,1,0:T(8,128)(2,1)} %slice.293), channel_id=1, source_target_pairs={{2,0},{4,2},{6,4},{3,1},{5,3},{7,5},{10,8},{12,10},{14,12},{11,9},... | collective-permute-start | bytes 196616 | tf_op jit(solution)/shard_map/ppermute | solution.py:19
  15.8 32.4 %collective-permute-start.2 = (bf16[4,1,64,128]{3,2,1,0:T(8,128)(2,1)}, bf16[4,1,64,128]{3,2,1,0:T(8,128)(2,1)}, u32[]{:S(2)}, u32[]{:S(2)}) collective-permute-start(bf16[4,1,64,128]{3,2,1,0:T(8,128)(2,1)} %slice.289), channel_id=1, source_target_pairs={{0,2},{2,4},{4,6},{1,3},{3,5},{5,7},{8,10},{10,12},{12,14},{9,11},... | collective-permute-start | bytes 196616 | tf_op jit(solution)/shard_map/ppermute | solution.py:17
  21.6 22.7 %collective-permute-start.5 = (bf16[4,8,1,128]{3,2,1,0:T(2,128)(2,1)}, bf16[4,8,1,128]{3,2,1,0:T(2,128)(2,1)}, u32[]{:S(2)}, u32[]{:S(2)}) collective-permute-start(bf16[4,8,1,128]{3,2,1,0:T(2,128)(2,1)} %slice.299), channel_id=1, source_target_pairs={{1,0},{3,2},{5,4},{7,6},{9,8},{11,10},{13,12},{15,14},{17,16},{19,... | collective-permute-start | bytes 24584 | tf_op jit(solution)/shard_map/ppermute | solution.py:19
  23.6 23.7 %collective-permute-start.4 = (bf16[4,8,1,128]{3,2,1,0:T(2,128)(2,1)}, bf16[4,8,1,128]{3,2,1,0:T(2,128)(2,1)S(1)}, u32[]{:S(2)}, u32[]{:S(2)}) collective-permute-start(bf16[4,8,1,128]{3,2,1,0:T(2,128)(2,1)} %slice.295), channel_id=1, source_target_pairs={{0,1},{2,3},{4,5},{6,7},{8,9},{10,11},{12,13},{14,15},{16,17},{18,... | collective-permute-start | bytes 24584 | tf_op jit(solution)/shard_map/ppermute | solution.py:17
  28.8 19.4 %collective-permute-start.1 = (bf16[1,8,64,128]{3,2,1,0:T(8,128)(2,1)}, bf16[1,8,64,128]{3,2,1,0:T(8,128)(2,1)}, u32[]{:S(2)}, u32[]{:S(2)}) collective-permute-start(bf16[1,8,64,128]{3,2,1,0:T(8,128)(2,1)} %get-tuple-element.20), channel_id=1, source_target_pairs={{8,0},{16,8},{24,16},{32,24},{40,32},{48,40},{56,48},{64,56},{72,6... | collective-permute-start | bytes 393224 | tf_op jit(solution)/shard_map/ppermute | solution.py:19
  35.8 4.3 %copy-start.10 = (bf16[6,4,8,64,128]{4,3,2,1,0:T(8,128)(2,1)}, bf16[6,4,8,64,128]{4,3,2,1,0:T(8,128)(2,1)S(1)}, u32[]{:S(2)}) copy-start(bf16[6,4,8,64,128]{4,3,2,1,0:T(8,128)(2,1)S(1)} %bitcast_dynamic-update-slice_fusion) | copy-start | bytes 9437188
  40.1 9.0 %copy-start.9 = (bf16[4,8,64,128]{3,2,1,0:T(8,128)(2,1)S(1)}, bf16[4,8,64,128]{3,2,1,0:T(8,128)(2,1)}, u32[]{:S(2)}) copy-start(bf16[4,8,64,128]{3,2,1,0:T(8,128)(2,1)} %param.5) | copy-start | bytes 1572868
  44.4 4.7 %collective-permute-start = (bf16[1,8,64,128]{3,2,1,0:T(8,128)(2,1)}, bf16[1,8,64,128]{3,2,1,0:T(8,128)(2,1)S(1)}, u32[]{:S(2)}, u32[]{:S(2)}) collective-permute-start(bf16[1,8,64,128]{3,2,1,0:T(8,128)(2,1)} %get-tuple-element.19), channel_id=1, source_target_pairs={{0,8},{8,16},{16,24},{24,32},{32,40},{40,48},{48,56},{56,64},{64,7... | collective-permute-start | bytes 393224 | tf_op jit(solution)/shard_map/ppermute | solution.py:17
  51.5 14.3 %copy-start.14 = (f32[4,8,64,128]{3,2,1,0:T(8,128)}, f32[4,8,64,128]{3,2,1,0:T(8,128)S(1)}, u32[]{:S(2)}) copy-start(f32[4,8,64,128]{3,2,1,0:T(8,128)S(1)} %get-tuple-element.13) | copy-start | bytes 3145732
  51.5 14.3 %copy-start.15 = (bf16[4,7,64,128]{3,2,1,0:T(8,128)(2,1)S(1)}, bf16[4,7,64,128]{3,2,1,0:T(8,128)(2,1)}, u32[]{:S(2)}) copy-start(bf16[4,7,64,128]{3,2,1,0:T(8,128)(2,1)} %slice.290) | copy-start | bytes 1376260
  51.5 14.3 %copy-start.16 = (bf16[4,7,64,128]{3,2,1,0:T(8,128)(2,1)S(1)}, bf16[4,7,64,128]{3,2,1,0:T(8,128)(2,1)}, u32[]{:S(2)}) copy-start(bf16[4,7,64,128]{3,2,1,0:T(8,128)(2,1)} %slice.292) | copy-start | bytes 1376260
  51.5 14.3 %copy-start.17 = (bf16[3,8,64,128]{3,2,1,0:T(8,128)(2,1)S(1)}, bf16[3,8,64,128]{3,2,1,0:T(8,128)(2,1)}, u32[]{:S(2)}) copy-start(bf16[3,8,64,128]{3,2,1,0:T(8,128)(2,1)} %get-tuple-element.21) | copy-start | bytes 1179652
  51.5 14.3 %copy-start.18 = (bf16[3,8,64,128]{3,2,1,0:T(8,128)(2,1)S(1)}, bf16[3,8,64,128]{3,2,1,0:T(8,128)(2,1)}, u32[]{:S(2)}) copy-start(bf16[3,8,64,128]{3,2,1,0:T(8,128)(2,1)} %get-tuple-element.22) | copy-start | bytes 1179652
  65.8 18.9 %slice-start = ((s8[6291456]{0:T(1024)(128)(4,1)}), s8[4194304]{0:T(1024)(128)(4,1)S(1)}, s32[]{:S(2)}) async-start(s8[6291456]{0:T(1024)(128)(4,1)} %bitcast.355), calls=%async_computation.2 | async-start | bytes 8388608
  66.7 12.9 %collective-permute-start.6 = (bf16[1,8,64,128]{3,2,1,0:T(8,128)(2,1)S(1)}, bf16[1,8,64,128]{3,2,1,0:T(8,128)(2,1)S(1)}, u32[]{:S(2)}, u32[]{:S(2)}) collective-permute-start(bf16[1,8,64,128]{3,2,1,0:T(8,128)(2,1)S(1)} %slice.301), channel_id=1, source_target_pairs={{8,0},{16,8},{24,16},{32,24},{40,32},{48,40},{56,48},{64,56},{72,6... | collective-permute-start | bytes 393224 | tf_op jit(solution)/shard_map/ppermute | solution.py:19
  69.3 14.4 %collective-permute-start.7 = (bf16[1,8,64,128]{3,2,1,0:T(8,128)(2,1)S(1)}, bf16[1,8,64,128]{3,2,1,0:T(8,128)(2,1)S(1)}, u32[]{:S(2)}, u32[]{:S(2)}) collective-permute-start(bf16[1,8,64,128]{3,2,1,0:T(8,128)(2,1)S(1)} %slice.302), channel_id=1, source_target_pairs={{0,8},{8,16},{16,24},{24,32},{32,40},{40,48},{48,56},{56,64},{64,7... | collective-permute-start | bytes 393224 | tf_op jit(solution)/shard_map/ppermute | solution.py:17
  72.5 53.9 %copy-start.24 = (f32[6,4,8,64]{3,2,1,0:T(8,128)}, f32[6,4,8,64]{3,2,1,0:T(8,128)S(1)}, u32[]{:S(2)}) copy-start(f32[6,4,8,64]{3,2,1,0:T(8,128)S(1)} %broadcast_divide_fusion) | copy-start | bytes 147460
  72.6 12.2 %slice-start.1 = ((s8[6291456]{0:T(1024)(128)(4,1)}), s8[2097152]{0:T(1024)(128)(4,1)S(1)}, s32[]{:S(2)}) async-start(s8[6291456]{0:T(1024)(128)(4,1)} %bitcast.355), calls=%async_computation.3 | async-start | bytes 4194304
  72.9 10.9 %collective-permute-start.8 = (bf16[4,1,64,128]{3,2,1,0:T(8,128)(2,1)S(1)}, bf16[4,1,64,128]{3,2,1,0:T(8,128)(2,1)S(1)}, u32[]{:S(2)}, u32[]{:S(2)}) collective-permute-start(bf16[4,1,64,128]{3,2,1,0:T(8,128)(2,1)S(1)} %slice.305), channel_id=1, source_target_pairs={{2,0},{4,2},{6,4},{3,1},{5,3},{7,5},{10,8},{12,10},{14,12},{11,9},... | collective-permute-start | bytes 196616 | tf_op jit(solution)/shard_map/ppermute | solution.py:19
  74.3 9.6 %collective-permute-start.9 = (bf16[4,1,64,128]{3,2,1,0:T(8,128)(2,1)S(1)}, bf16[4,1,64,128]{3,2,1,0:T(8,128)(2,1)S(1)}, u32[]{:S(2)}, u32[]{:S(2)}) collective-permute-start(bf16[4,1,64,128]{3,2,1,0:T(8,128)(2,1)S(1)} %slice.306), channel_id=1, source_target_pairs={{0,2},{2,4},{4,6},{1,3},{3,5},{5,7},{8,10},{10,12},{12,14},{9,11},... | collective-permute-start | bytes 196616 | tf_op jit(solution)/shard_map/ppermute | solution.py:17
  78.3 5.7 %collective-permute-start.10 = (bf16[4,8,1,128]{3,2,1,0:T(2,128)(2,1)S(1)}, bf16[4,8,1,128]{3,2,1,0:T(2,128)(2,1)S(1)}, u32[]{:S(2)}, u32[]{:S(2)}) collective-permute-start(bf16[4,8,1,128]{3,2,1,0:T(2,128)(2,1)S(1)} %slice.309), channel_id=1, source_target_pairs={{1,0},{3,2},{5,4},{7,6},{9,8},{11,10},{13,12},{15,14},{17,16},{19,... | collective-permute-start | bytes 24584 | tf_op jit(solution)/shard_map/ppermute | solution.py:19
  79.6 4.8 %collective-permute-start.11 = (bf16[4,8,1,128]{3,2,1,0:T(2,128)(2,1)S(1)}, bf16[4,8,1,128]{3,2,1,0:T(2,128)(2,1)S(1)}, u32[]{:S(2)}, u32[]{:S(2)}) collective-permute-start(bf16[4,8,1,128]{3,2,1,0:T(2,128)(2,1)S(1)} %slice.310), channel_id=1, source_target_pairs={{0,1},{2,3},{4,5},{6,7},{8,9},{10,11},{12,13},{14,15},{16,17},{18,... | collective-permute-start | bytes 24584 | tf_op jit(solution)/shard_map/ppermute | solution.py:17
  84.7 3.8 %copy-start.23 = (f32[6,4,8,64]{3,2,1,0:T(8,128)S(1)}, f32[6,4,8,64]{3,2,1,0:T(8,128)}, u32[]{:S(2)}) copy-start(f32[6,4,8,64]{3,2,1,0:T(8,128)} %broadcast_divide_fusion.1) | copy-start | bytes 147460
  88.5 5.5 %copy-start.1 = (bf16[6,4,8,64,128]{4,3,2,1,0:T(8,128)(2,1)S(1)}, bf16[6,4,8,64,128]{4,3,2,1,0:T(8,128)(2,1)}, u32[]{:S(2)}) copy-start(bf16[6,4,8,64,128]{4,3,2,1,0:T(8,128)(2,1)} %param.8) | copy-start | bytes 9437188
  95.2 1.4 copy-start.8
  95.2 1.5 copy-start.5
  95.7 1.2 copy-start.6
  96.6 13.8 %copy-start.19 = (bf16[4,8,64,128]{3,2,1,0:T(8,128)(2,1)}, bf16[4,8,64,128]{3,2,1,0:T(8,128)(2,1)S(1)}, u32[]{:S(2)}) copy-start(bf16[4,8,64,128]{3,2,1,0:T(8,128)(2,1)S(1)} %multiply_convert_fusion.5) | copy-start | bytes 1572868
  96.9 7.9 %copy-start.13 = (bf16[6,4,8,64,128]{4,3,2,1,0:T(8,128)(2,1)S(1)}, bf16[6,4,8,64,128]{4,3,2,1,0:T(8,128)(2,1)}, u32[]{:S(2)}) copy-start(bf16[6,4,8,64,128]{4,3,2,1,0:T(8,128)(2,1)} %copy-done.12) | copy-start | bytes 9437188
  96.9 25.7 %slice-start.2 = ((s8[6291456]{0:T(1024)(128)(4,1)}), s8[2097152]{0:T(1024)(128)(4,1)S(1)}, s32[]{:S(2)}) async-start(s8[6291456]{0:T(1024)(128)(4,1)} %bitcast.357), calls=%async_computation.4 | async-start | bytes 4194304
  98.1 23.4 %collective-permute-start.13 = (bf16[1,8,64,128]{3,2,1,0:T(8,128)(2,1)S(1)}, bf16[1,8,64,128]{3,2,1,0:T(8,128)(2,1)S(1)}, u32[]{:S(2)}, u32[]{:S(2)}) collective-permute-start(bf16[1,8,64,128]{3,2,1,0:T(8,128)(2,1)S(1)} %slice.320), channel_id=1, source_target_pairs={{0,8},{8,16},{16,24},{24,32},{32,40},{40,48},{48,56},{56,64},{64,7... | collective-permute-start | bytes 393224 | tf_op jit(solution)/shard_map/ppermute | solution.py:17
  102.3 20.2 %slice-start.3 = ((s8[6291456]{0:T(1024)(128)(4,1)}), s8[4194304]{0:T(1024)(128)(4,1)S(1)}, s32[]{:S(2)}) async-start(s8[6291456]{0:T(1024)(128)(4,1)} %bitcast.357), calls=%async_computation.5 | async-start | bytes 8388608
  102.4 15.1 %collective-permute-start.12 = (bf16[1,8,64,128]{3,2,1,0:T(8,128)(2,1)S(1)}, bf16[1,8,64,128]{3,2,1,0:T(8,128)(2,1)S(1)}, u32[]{:S(2)}, u32[]{:S(2)}) collective-permute-start(bf16[1,8,64,128]{3,2,1,0:T(8,128)(2,1)S(1)} %slice.319), channel_id=1, source_target_pairs={{8,0},{16,8},{24,16},{32,24},{40,32},{48,40},{56,48},{64,56},{72,6... | collective-permute-start | bytes 393224 | tf_op jit(solution)/shard_map/ppermute | solution.py:19
  110.5 11.0 %slice-start.4 = ((bf16[4,8,64,128]{3,2,1,0:T(8,128)(2,1)}), bf16[3,8,64,128]{3,2,1,0:T(8,128)(2,1)S(1)}, s32[]{:S(2)}) async-start(bf16[4,8,64,128]{3,2,1,0:T(8,128)(2,1)} %copy-done.19), calls=%async_computation.6 | async-start | bytes 786432 | tf_op jit(solution)/shard_map/slice | solution.py:99
  110.8 10.8 %collective-permute-start.14 = (bf16[4,1,64,128]{3,2,1,0:T(8,128)(2,1)S(1)}, bf16[4,1,64,128]{3,2,1,0:T(8,128)(2,1)S(1)}, u32[]{:S(2)}, u32[]{:S(2)}) collective-permute-start(bf16[4,1,64,128]{3,2,1,0:T(8,128)(2,1)S(1)} %slice.323), channel_id=1, source_target_pairs={{2,0},{4,2},{6,4},{3,1},{5,3},{7,5},{10,8},{12,10},{14,12},{11,9},... | collective-permute-start | bytes 196616 | tf_op jit(solution)/shard_map/ppermute | solution.py:19
  112.1 9.6 %collective-permute-start.15 = (bf16[4,1,64,128]{3,2,1,0:T(8,128)(2,1)S(1)}, bf16[4,1,64,128]{3,2,1,0:T(8,128)(2,1)S(1)}, u32[]{:S(2)}, u32[]{:S(2)}) collective-permute-start(bf16[4,1,64,128]{3,2,1,0:T(8,128)(2,1)S(1)} %slice.324), channel_id=1, source_target_pairs={{0,2},{2,4},{4,6},{1,3},{3,5},{5,7},{8,10},{10,12},{12,14},{9,11},... | collective-permute-start | bytes 196616 | tf_op jit(solution)/shard_map/ppermute | solution.py:17
  116.1 5.7 %collective-permute-start.16 = (bf16[4,8,1,128]{3,2,1,0:T(2,128)(2,1)S(1)}, bf16[4,8,1,128]{3,2,1,0:T(2,128)(2,1)S(1)}, u32[]{:S(2)}, u32[]{:S(2)}) collective-permute-start(bf16[4,8,1,128]{3,2,1,0:T(2,128)(2,1)S(1)} %slice.327), channel_id=1, source_target_pairs={{1,0},{3,2},{5,4},{7,6},{9,8},{11,10},{13,12},{15,14},{17,16},{19,... | collective-permute-start | bytes 24584 | tf_op jit(solution)/shard_map/ppermute | solution.py:19
  117.4 4.8 %collective-permute-start.17 = (bf16[4,8,1,128]{3,2,1,0:T(2,128)(2,1)S(1)}, bf16[4,8,1,128]{3,2,1,0:T(2,128)(2,1)S(1)}, u32[]{:S(2)}, u32[]{:S(2)}) collective-permute-start(bf16[4,8,1,128]{3,2,1,0:T(2,128)(2,1)S(1)} %slice.328), channel_id=1, source_target_pairs={{0,1},{2,3},{4,5},{6,7},{8,9},{10,11},{12,13},{14,15},{16,17},{18,... | collective-permute-start | bytes 24584 | tf_op jit(solution)/shard_map/ppermute | solution.py:17
  122.5 3.9 %copy-start.7 = (bf16[6,4,8,64,128]{4,3,2,1,0:T(8,128)(2,1)}, bf16[6,4,8,64,128]{4,3,2,1,0:T(8,128)(2,1)S(1)}, u32[]{:S(2)}) copy-start(bf16[6,4,8,64,128]{4,3,2,1,0:T(8,128)(2,1)S(1)} %fusion.66) | copy-start | bytes 9437188
  122.6 3.9 %copy-start.11 = (bf16[6,4,8,64,128]{4,3,2,1,0:T(8,128)(2,1)S(1)}, bf16[6,4,8,64,128]{4,3,2,1,0:T(8,128)(2,1)}, u32[]{:S(2)}) copy-start(bf16[6,4,8,64,128]{4,3,2,1,0:T(8,128)(2,1)} %copy-done.10) | copy-start | bytes 9437188
  132.7 41.6 %all-to-all-start = ((f32[256,1,384]{2,1,0:T(1,128)}), f32[256,1,384]{2,1,0:T(1,128)}, u32[]{:S(2)}, u32[]{:S(2)}) async-start(f32[256,1,384]{2,1,0:T(1,128)} %bitcast.75), calls=%async_computation | async-start | bytes 786432 | tf_op jit(solution)/shard_map/all_to_all | solution.py:159
  156.7 27.0 %copy-start.2 = (bf16[6,4,8,64,128]{4,3,2,1,0:T(8,128)(2,1)S(1)}, bf16[6,4,8,64,128]{4,3,2,1,0:T(8,128)(2,1)}, u32[]{:S(2)}) copy-start(bf16[6,4,8,64,128]{4,3,2,1,0:T(8,128)(2,1)} %param.8) | copy-start | bytes 9437188
  176.5 24.9 %all-to-all-start.1 = ((f32[256,1,384]{2,1,0:T(1,128)}), f32[256,1,384]{2,1,0:T(1,128)}, u32[]{:S(2)}, u32[]{:S(2)}) async-start(f32[256,1,384]{2,1,0:T(1,128)} %broadcast_in_dim.11), calls=%async_computation.1 | async-start | bytes 786432 | tf_op jit(solution)/shard_map/all_to_all | solution.py:161
  183.8 17.7 %copy-start.22 = (f32[6,128,128]{2,1,0:T(8,128)S(1)}, f32[6,128,128]{2,1,0:T(8,128)}, u32[]{:S(2)}) copy-start(f32[6,128,128]{2,1,0:T(8,128)} %param.6) | copy-start | bytes 1179652

commit v2 on v1

--- a/solution.py
+++ b/solution.py
@@ -44,15 +44,22 @@
 
 
 def trade(low_face, high_face, axis_dim):
-    packed = jnp.concatenate([low_face, high_face], axis=axis_dim)
-    if axis_dim == 0:
-        rims = extended(packed, (("gx", 0),), 1)
-    elif axis_dim == 1:
-        rims = extended(packed, (("gy", 1),), 1)
+    axis = ("gx", "gy", "gz")[axis_dim]
+    count = lax.axis_size(axis)
+    odd = lax.axis_index(axis) % 2 == 1
+    first = lax.ppermute(
+        jnp.where(odd, low_face, high_face), axis, [(i, i ^ 1) for i in range(count)]
+    )
+    if count > 2:
+        second = lax.ppermute(
+            jnp.where(odd, high_face, low_face),
+            axis,
+            [(i, i + 1 if i % 2 == 1 else i - 1) for i in range(1, count - 1)],
+        )
     else:
-        rims = extended(packed, (("gz", 2),), 1)
-    lower = lax.slice_in_dim(rims, 0, 1, axis=axis_dim)
-    upper = lax.slice_in_dim(rims, 3, 4, axis=axis_dim)
+        second = jnp.zeros_like(first)
+    lower = jnp.where(odd, first, second)
+    upper = jnp.where(odd, second, first)
     return (lower, upper)
 
 

time: 204 us -> 188 us (0.922)
  starting transfers between devices: 84.8 us -> 57 us
  other arithmetic: 52.5 us -> 56.9 us
  waiting for transfers between devices: 21.3 us -> 25.2 us
  matrix products: 31 us -> 34.8 us
    ppermute x18 -> x15, starting transfers between devices: 53.6 us -> 28 us  [the longest x6 14.3 us: trade(): lax.ppermute(jnp.where(odd, high_face, low_face), axis, [(i, i + 1 if i %...]
    dot_general x2, matrix products: 6.2 us -> 10.1 us  [send_terms(): jnp.einsum('dxyzk,dkl->dxyzl', hidden_b, weights_b, preferred_element_typ...]
    ppermute x18 -> x15, waiting for transfers between devices: 0.86 us -> 4.69 us  [the longest x6 4.67 us: trade(): lax.ppermute(jnp.where(odd, high_face, low_face), axis, [(i, i + 1 if i %...]
    slice x17 -> x0, local copies, waits for them, and re-layouts: 3.39 us -> none  [the longest x3 1.96 us: spread(): lax.slice_in_dim(plus, length - 1, length, axis=axis_dim)]
    select_n x3 -> x1, other arithmetic: 2.54 us -> 0.04 us  [spread(): upper = jnp.where(upper_edge[axis_dim], ones, upper)]
    select_n x0 -> x15, other arithmetic: none -> 2.48 us  [the longest x9 2.33 us: trade(): jnp.where(odd, low_face, high_face)]
    another operation x1, other arithmetic: 0.22 us -> 2.56 us  [send_terms(): hidden_b = jnp.stack(hidden).astype(jnp.bfloat16)]
    all_to_all x1, starting transfers between devices: 24 us -> 21.8 us  [all_sum(): lax.all_to_all(rows, axes, 0, 0, tiled=True)]
  transfers between devices with their start and end apart: 20 -> 17, of which waited for: 4 -> 4; matrix products, arithmetic and copies ran while one was open for 18% -> 18% of each run, Pallas kernels for 0% -> 0%
where the time goes in v2:
time: 188 us; the launch traced here: 187 us
  starting transfers between devices  57 us (30%)
  other arithmetic  56.9 us (30%)
  matrix products  34.8 us (19%)
  waiting for transfers between devices  25.2 us (13%)
  local copies, waits for them, and re-layouts  11.8 us (6%)
    all_to_all x1, starting transfers between devices, all_sum(): lax.all_to_all(rows, axes, 0, 0, tiled=True)  21.8 us
    sub x1, other arithmetic, belief_adjoint(): cotangent - jnp.sum(cotangent * belief, axis=-1, keepdims=True)  14.3 us
    ppermute x6, starting transfers between devices, trade(): lax.ppermute(jnp.where(odd, high_face, low_face), axis, [(i, i + 1 if i %...  14.3 us
    ppermute x9, starting transfers between devices, trade(): lax.ppermute(jnp.where(odd, low_face, high_face), axis, [(i, i ^ 1) for i...  13.7 us
    dot_general x2, matrix products, local_adjoint(): jnp.einsum('dxyzl,dkl->dxyzk', grad_out, weights_b, preferred_element_typ...  12.8 us
    dot_general x2, matrix products, local_adjoint(): jnp.einsum('dxyzk,dxyzl->dkl', hidden_b, grad_out, preferred_element_type...  11.9 us
    all_to_all x1, waiting for transfers between devices, all_sum(): lax.all_to_all(spread_out, axes, 0, 0, tiled=True).reshape(value.shape)  10.3 us
    all_to_all x1, waiting for transfers between devices, all_sum(): lax.all_to_all(rows, axes, 0, 0, tiled=True)  10.2 us
  transfers between devices with their start and end apart: 17, of which 4 were waited for; matrix products, arithmetic and copies ran while one was open for 18% of the time, Pallas kernels for 0%

profile of v2, /device:TPU:1, one launch (start us, length us, event | category | flops | bytes accessed | tf_op | source)
XLA Modules:
  0.0 187.4 jit_solution(1983745634819132243)
XLA Ops:
  0.7 4.7 %bitcast_dynamic-update-slice_fusion.5 = (bf16[6,4,8,64,128]{4,3,2,1,0:T(8,128)(2,1)S(1)}, f32[4,8,64,128]{3,2,1,0:T(8,128)S(1)}, bf16[6,4,8,64,128]{4,3,2,1,0:T(8,128)(2,1)S(1)}, f32[4,8,64,128]{3,2,1,0:T(8,128)S(1)}) fusion(bf16[6,4,8,64,128]{4,3,2,1,0:T(8,128)(2,1)} %param.7, bf16[4,8,64,128]{3,2,1,0:T(8,128)(2,1)} %param.5, ...), kind=kLoop, calls=%fused_computation.152 | loop fusion | flops 7602174 | bytes 9961472
  5.4 0.2 bitcast_dynamic-update-slice_fusion.10
  5.6 0.2 bitcast_dynamic-update-slice_fusion.9
  5.8 0.2 bitcast_dynamic-update-slice_fusion.8
  6.1 0.2 bitcast_dynamic-update-slice_fusion.7
  6.3 1.8 copy-done.4
  8.1 0.2 bitcast_dynamic-update-slice_fusion.4
  8.3 0.2 bitcast_dynamic-update-slice_fusion.3
  8.5 0.2 bitcast_dynamic-update-slice_fusion.2
  8.7 0.2 bitcast_dynamic-update-slice_fusion.1
  8.9 1.7 copy-done.11
  10.7 2.6 %bitcast_dynamic-update-slice_fusion = (bf16[6,4,8,64,128]{4,3,2,1,0:T(8,128)(2,1)}, bf16[6,4,8,64,128]{4,3,2,1,0:T(8,128)(2,1)}) fusion(bf16[6,4,8,64,128]{4,3,2,1,0:T(8,128)(2,1)} %copy-done.11, f32[4,8,64,128]{3,2,1,0:T(8,128)S(1)} %get-tuple-element.3, bf16[6,4,8,64,128]{4,3,2,1,0:T(8,128)(2,1)} %param.7, bf16[6,4,8,64,128]{4,3,2,1,0:T(8,128)(2,1)} %copy-done.13, ...), kind=kLoop, calls=%fused_computation.147 | loop fusion | flops 1572864 | bytes 4194304 | tf_op jit(solution)/shard_map/stack | solution.py:37
  13.2 3.8 %fusion.77 = (f32[6,4,8,64]{3,2,1,0:T(8,128)S(1)}, f32[6,4,8,64,128]{4,3,2,1,0:T(8,128)S(1)}) fusion(bf16[6,4,8,64,128]{4,3,2,1,0:T(8,128)(2,1)} %get-tuple-element.68, bf16[6,128,128,1,1]{2,1,4,3,0:T(8,128)(2,1)S(1)} %fusion.68), kind=kOutput, calls=%fused_computation.208 | convolution fusion | flops 404213760 | bytes 9682944 | tf_op jit(solution)/shard_map/dxyzk,dkl->dxyzl/dot_general | solution.py:38
  17.0 2.0 %fusion.13 = bf16[6,4,8,64,128]{4,3,2,1,0:T(8,128)(2,1)S(1)} fusion(f32[6,4,8,64]{3,2,1,0:T(8,128)S(1)} %get-tuple-element.62, f32[6,4,8,64,128]{4,3,2,1,0:T(8,128)S(1)} %get-tuple-element.63), kind=kLoop, calls=%fused_computation.18 | loop fusion | flops 4718592 | bytes 9486336 | tf_op jit(solution)/shard_map/convert.29
  19.0 0.6 copy-done.3
  19.7 0.8 select_bitcast_fusion.1
  20.4 3.2 %collective-permute-start = (bf16[1,8,64,128]{3,2,1,0:T(8,128)(2,1)}, bf16[1,8,64,128]{3,2,1,0:T(8,128)(2,1)}, u32[]{:S(2)}, u32[]{:S(2)}) collective-permute-start(bf16[1,8,64,128]{3,2,1,0:T(8,128)(2,1)} %get-tuple-element.21), channel_id=1, source_target_pairs={{0,8},{8,0},{16,24},{24,16},{32,40},{40,32},{48,56},{56,48},{64,72... | collective-permute-start | bytes 393224 | tf_op jit(solution)/shard_map/ppermute | solution.py:50
  23.6 1.9 %collective-permute-start.1 = (bf16[1,8,64,128]{3,2,1,0:T(8,128)(2,1)}, bf16[1,8,64,128]{3,2,1,0:T(8,128)(2,1)}, u32[]{:S(2)}, u32[]{:S(2)}) collective-permute-start(bf16[1,8,64,128]{3,2,1,0:T(8,128)(2,1)} %get-tuple-element.22), channel_id=1, source_target_pairs={{8,16},{16,8},{24,32},{32,24},{40,48},{48,40},{56,64},{64,56},{72,... | collective-permute-start | bytes 393224 | tf_op jit(solution)/shard_map/ppermute | solution.py:54
  25.8 0.8 broadcast_select_fusion.17
  26.6 0.7 collective-permute-start.2
  27.2 1.3 collective-permute-start.3
  28.5 0.6 broadcast_select_fusion.27
  29.2 1.6 collective-permute-start.4
  30.8 2.1 %slice_bitcast_fusion.17 = (bf16[3,8,64,128]{3,2,1,0:T(8,128)(2,1)}, bf16[3,8,64,128]{3,2,1,0:T(8,128)(2,1)}) fusion(bf16[6,4,8,64,128]{4,3,2,1,0:T(8,128)(2,1)} %copy-done.8), kind=kLoop, calls=%fused_computation.161 | loop fusion | bytes 1572864 | tf_op jit(solution)/shard_map/slice | solution.py:82
  32.9 0.6 broadcast_divide_fusion.1
  33.5 6.3 %fusion.78 = (f32[6,4,8,64]{3,2,1,0:T(8,128)S(1)}, f32[6,4,8,64,128]{4,3,2,1,0:T(8,128)}) fusion(bf16[6,4,8,64,128]{4,3,2,1,0:T(8,128)(2,1)} %get-tuple-element.67, bf16[6,128,128,1,1]{2,1,4,3,0:T(8,128)(2,1)S(1)} %fusion.68), kind=kOutput, calls=%fused_computation.209 | convolution fusion | flops 404213760 | bytes 9682944 | tf_op jit(solution)/shard_map/dxyzk,dkl->dxyzl/dot_general | solution.py:38
  39.8 0.7 broadcast_divide_fusion
  40.7 1.8 slice.286
  42.5 1.8 slice.287
  44.4 0.9 select_select_fusion.3
  45.3 1.0 select_select_fusion.1
  46.3 2.3 %fusion.72 = (f32[4,8,64]{2,1,0:T(8,128)S(1)}, f32[4,8,64,128]{3,2,1,0:T(8,128)S(1)}) fusion(bf16[4,8,64,128]{3,2,1,0:T(8,128)(2,1)S(1)} %copy-done.10, bf16[4,8,1,128]{3,2,1,0:T(2,128)(2,1)S(1)} %get-tuple-element.60, bf16[4,8,63,128]{3,2,1,0:T(8,128)(2,1)S(1)} %slice.293, bf16[4,8,63,128]{3,2,1,0:T(8,128)(2,1)} %bitcast.360, ...), kind=kLoop, calls=%fused_computation.207 | loop fusion | flops 8386560 | bytes 4726784 | tf_op jit(solution)/shard_map/reduce_sum | solution.py:121
  48.6 14.3 %fusion.36 = (bf16[4,8,64,128]{3,2,1,0:T(8,128)(2,1)S(1)}, f32[4,8,64,128]{3,2,1,0:T(8,128)S(1)}, f32[4,8,64,128]{3,2,1,0:T(8,128)}) fusion(bf16[4,8,63,128]{3,2,1,0:T(8,128)(2,1)} %bitcast.361, bf16[4,8,1,128]{3,2,1,0:T(2,128)(2,1)S(1)} %get-tuple-element.61, f32[4,8,64,128]{3,2,1,0:T(8,128)S(1)} %get-tuple-element.13, ...), kind=kOutput, calls=%fused_computation.74 | output fusion | flops 4196479 | bytes 5775360 | tf_op jit(solution)/shard_map/sub | solution.py:123
  63.0 0.7 fusion.37
  64.3 0.8 collective-permute-start.7
  65.1 4.3 %collective-permute-start.8 = (bf16[4,1,64,128]{3,2,1,0:T(8,128)(2,1)S(1)}, bf16[4,1,64,128]{3,2,1,0:T(8,128)(2,1)S(1)}, u32[]{:S(2)}, u32[]{:S(2)}) collective-permute-start(bf16[4,1,64,128]{3,2,1,0:T(8,128)(2,1)S(1)} %get-tuple-element.36), channel_id=1, source_target_pairs={{0,2},{2,0},{4,6},{6,4},{1,3},{3,1},{5,7},{7,5},{8,10},{10,8},{12,... | collective-permute-start | bytes 196616 | tf_op jit(solution)/shard_map/ppermute | solution.py:50
  69.4 5.1 %collective-permute-start.5 = (bf16[1,8,64,128]{3,2,1,0:T(8,128)(2,1)S(1)}, bf16[1,8,64,128]{3,2,1,0:T(8,128)(2,1)S(1)}, u32[]{:S(2)}, u32[]{:S(2)}) collective-permute-start(bf16[1,8,64,128]{3,2,1,0:T(8,128)(2,1)S(1)} %get-tuple-element.39), channel_id=1, source_target_pairs={{8,16},{16,8},{24,32},{32,24},{40,48},{48,40},{56,64},{64,56},{72,... | collective-permute-start | bytes 393224 | tf_op jit(solution)/shard_map/ppermute | solution.py:54
  74.4 0.3 collective-permute-start.6
  74.8 2.2 %collective-permute-done.5 = bf16[1,8,64,128]{3,2,1,0:T(8,128)(2,1)S(1)} collective-permute-done((bf16[1,8,64,128]{3,2,1,0:T(8,128)(2,1)S(1)}, bf16[1,8,64,128]{3,2,1,0:T(8,128)(2,1)S(1)}, u32[]{:S(2)}, u32[]{:S(2)}) %collective-permute-start.5) | collective-permute-done | bytes 131104 | tf_op jit(solution)/shard_map/ppermute | solution.py:54
  77.5 0.2 fusion.60
  77.8 3.8 %fusion.1 = f32[6,4,8,64]{3,2,1,0:T(8,128)S(1)} fusion(bf16[6,4,8,64,128]{4,3,2,1,0:T(8,128)(2,1)S(1)} %fusion.60, f32[6,4,8,64]{3,2,1,0:T(8,128)S(1)} %get-tuple-element.62, f32[6,4,8,64,128]{4,3,2,1,0:T(8,128)S(1)} %bitcast.356), kind=kLoop, calls=%fused_computation.5 | loop fusion | flops 7852032 | bytes 9535488 | tf_op jit(solution)/shard_map/reduce_sum | solution.py:132
  81.6 5.7 %fusion.17 = f32[6,128,128]{2,1,0:T(8,128)S(1)} fusion(bf16[6,4,8,64,128]{4,3,2,1,0:T(8,128)(2,1)S(1)} %copy-done.14, bf16[6,4,8,64,128]{4,3,2,1,0:T(8,128)(2,1)S(1)} %fusion.60, f32[6,4,8,64]{3,2,1,0:T(8,128)S(1)} %broadcast_multiply_fusion.1, f32[6,4,8,64]{3,2,1,0:T(8,128)S(1)} %copy-done.27), kind=kOutput, calls=%fused_computation.67 | convolution fusion | flops 408944640 | bytes 6782976 | tf_op jit(solution)/shard_map/dxyzk,dxyzl->dkl/dot_general | solution.py:134
  87.2 5.5 %fusion.79 = f32[6,4,8,64,128]{4,3,2,1,0:T(8,128)S(1)} fusion(bf16[6,128,128,1,1]{2,1,4,3,0:T(8,128)(2,1)S(1)} %fusion.68, bf16[6,4,8,64,128]{4,3,2,1,0:T(8,128)(2,1)S(1)} %fusion.60, f32[6,4,8,64]{3,2,1,0:T(8,128)S(1)} %broadcast_multiply_fusion.1, f32[6,4,8,64]{3,2,1,0:T(8,128)S(1)} %copy-done.27), kind=kOutput, calls=%fused_computation.210 | convolution fusion | flops 408944640 | bytes 9732096 | tf_op jit(solution)/shard_map/dxyzl,dkl->dxyzk/dot_general | solution.py:137
  92.8 1.1 multiply_convert_fusion.1
  93.9 0.5 multiply_convert_fusion
  94.4 0.4 collective-permute-start.14
  94.8 1.0 multiply_convert_fusion.5
  95.8 1.2 multiply_convert_fusion.2
  97.4 0.8 collective-permute-start.12
  98.2 2.9 %collective-permute-start.13 = (bf16[4,1,64,128]{3,2,1,0:T(8,128)(2,1)S(1)}, bf16[4,1,64,128]{3,2,1,0:T(8,128)(2,1)S(1)}, u32[]{:S(2)}, u32[]{:S(2)}) collective-permute-start(bf16[4,1,64,128]{3,2,1,0:T(8,128)(2,1)S(1)} %get-tuple-element.27), channel_id=1, source_target_pairs={{0,2},{2,0},{4,6},{6,4},{1,3},{3,1},{5,7},{7,5},{8,10},{10,8},{12,... | collective-permute-start | bytes 196616 | tf_op jit(solution)/shard_map/ppermute | solution.py:50
  101.2 4.5 %collective-permute-start.10 = (bf16[1,8,64,128]{3,2,1,0:T(8,128)(2,1)S(1)}, bf16[1,8,64,128]{3,2,1,0:T(8,128)(2,1)S(1)}, u32[]{:S(2)}, u32[]{:S(2)}) collective-permute-start(bf16[1,8,64,128]{3,2,1,0:T(8,128)(2,1)S(1)} %get-tuple-element.30), channel_id=1, source_target_pairs={{8,16},{16,8},{24,32},{32,24},{40,48},{48,40},{56,64},{64,56},{72,... | collective-permute-start | bytes 393224 | tf_op jit(solution)/shard_map/ppermute | solution.py:54
  105.8 2.4 %collective-permute-done.10 = bf16[1,8,64,128]{3,2,1,0:T(8,128)(2,1)S(1)} collective-permute-done((bf16[1,8,64,128]{3,2,1,0:T(8,128)(2,1)S(1)}, bf16[1,8,64,128]{3,2,1,0:T(8,128)(2,1)S(1)}, u32[]{:S(2)}, u32[]{:S(2)}) %collective-permute-start.10) | collective-permute-done | bytes 131104 | tf_op jit(solution)/shard_map/ppermute | solution.py:54
  108.7 0.2 fusion.66
  109.0 3.8 %fusion.4 = f32[6,4,8,64]{3,2,1,0:T(8,128)S(1)} fusion(bf16[6,4,8,64,128]{4,3,2,1,0:T(8,128)(2,1)S(1)} %fusion.66, f32[6,4,8,64,128]{4,3,2,1,0:T(8,128)S(1)} %bitcast.358, f32[6,4,8,64]{3,2,1,0:T(8,128)S(1)} %get-tuple-element.65), kind=kLoop, calls=%fused_computation.8 | loop fusion | flops 7852032 | bytes 9535488 | tf_op jit(solution)/shard_map/reduce_sum | solution.py:132
  112.9 6.3 %fusion.27 = f32[6,128,128]{2,1,0:T(8,128)} fusion(f32[6,128,128]{2,1,0:T(8,128)S(1)} %fusion.17, bf16[6,4,8,64,128]{4,3,2,1,0:T(8,128)(2,1)S(1)} %copy-done.12, bf16[6,4,8,64,128]{4,3,2,1,0:T(8,128)(2,1)S(1)} %fusion.66, f32[6,4,8,64]{3,2,1,0:T(8,128)S(1)} %broadcast_multiply_fusion, f32[6,4,8,64]{3,2,1,0:T(8,128)S(1)} %copy-done.26), kind=kOutput, calls=%fused_computation.69 | convolution fusion | flops 409042944 | bytes 7176192 | tf_op jit(solution)/shard_map/dxyzk,dxyzl->dkl/dot_general | solution.py:134
  119.2 21.8 %all-to-all-start = ((f32[256,1,384]{2,1,0:T(1,128)}), f32[256,1,384]{2,1,0:T(1,128)}, u32[]{:S(2)}, u32[]{:S(2)}) async-start(f32[256,1,384]{2,1,0:T(1,128)} %bitcast.75), calls=%async_computation | async-start | bytes 786432 | tf_op jit(solution)/shard_map/all_to_all | solution.py:166
  141.0 7.3 %fusion.80 = f32[6,4,8,64,128]{4,3,2,1,0:T(8,128)} fusion(bf16[6,128,128,1,1]{2,1,4,3,0:T(8,128)(2,1)S(1)} %fusion.68, bf16[6,4,8,64,128]{4,3,2,1,0:T(8,128)(2,1)} %copy-done.7, f32[6,4,8,64]{3,2,1,0:T(8,128)S(1)} %broadcast_multiply_fusion, f32[6,4,8,64]{3,2,1,0:T(8,128)S(1)} %copy-done.26), kind=kOutput, calls=%fused_computation.211 | convolution fusion | flops 408944640 | bytes 9732096 | tf_op jit(solution)/shard_map/dxyzl,dkl->dxyzk/dot_general | solution.py:137
  148.3 10.2 %all-to-all-done = f32[256,1,384]{2,1,0:T(1,128)} async-done(((f32[256,1,384]{2,1,0:T(1,128)}), f32[256,1,384]{2,1,0:T(1,128)}, u32[]{:S(2)}, u32[]{:S(2)}) %all-to-all-start) | async-done | bytes 393248 | tf_op jit(solution)/shard_map/all_to_all | solution.py:166
  158.5 1.3 reduce_sum.69
  159.8 1.0 broadcast_in_dim.11
  160.7 7.2 %all-to-all-start.1 = ((f32[256,1,384]{2,1,0:T(1,128)}), f32[256,1,384]{2,1,0:T(1,128)}, u32[]{:S(2)}, u32[]{:S(2)}) async-start(f32[256,1,384]{2,1,0:T(1,128)} %broadcast_in_dim.11), calls=%async_computation.1 | async-start | bytes 786432 | tf_op jit(solution)/shard_map/all_to_all | solution.py:168
  168.0 7.4 %fusion.46 = f32[4,8,64,128]{3,2,1,0:T(8,128)} fusion(f32[6,4,8,64,128]{4,3,2,1,0:T(8,128)} %fusion.80, f32[4,8,64,128]{3,2,1,0:T(8,128)} %copy-done.5, f32[4,8,64,128]{3,2,1,0:T(8,128)} %get-tuple-element.64, f32[4,8,64,128]{3,2,1,0:T(8,128)} %copy-done.15, bf16[4,8,64,128]{3,2,1,0:T(8,128)(2,1)} %param.5, f32[4,8,64,128]{3,2,1,0:T(8,128)} %copy-done.9, ...), kind=kLoop, calls=%fused_computation.84 | loop fusion | flops 11010048 | bytes 19398656 | tf_op jit(solution)/shard_map/mul | solution.py:207
  175.4 10.3 %all-to-all-done.1 = f32[256,1,384]{2,1,0:T(1,128)} async-done(((f32[256,1,384]{2,1,0:T(1,128)}), f32[256,1,384]{2,1,0:T(1,128)}, u32[]{:S(2)}, u32[]{:S(2)}) %all-to-all-start.1) | async-done | bytes 393248 | tf_op jit(solution)/shard_map/all_to_all | solution.py:168
  185.6 1.8 exponential_multiply_fusion
  (117 shorter events, 2.4 us)
Async XLA Ops:
  0.6 4.7 %copy-start = (bf16[6,4,8,64,128]{4,3,2,1,0:T(8,128)(2,1)S(1)}, bf16[6,4,8,64,128]{4,3,2,1,0:T(8,128)(2,1)}, u32[]{:S(2)}) copy-start(bf16[6,4,8,64,128]{4,3,2,1,0:T(8,128)(2,1)} %param.8) | copy-start | bytes 9437188
  5.6 2.5 %copy-start.4 = (bf16[6,4,8,64,128]{4,3,2,1,0:T(8,128)(2,1)S(1)}, bf16[6,4,8,64,128]{4,3,2,1,0:T(8,128)(2,1)}, u32[]{:S(2)}) copy-start(bf16[6,4,8,64,128]{4,3,2,1,0:T(8,128)(2,1)} %param.7) | copy-start | bytes 9437188
  6.3 2.4 %copy-start.13 = (bf16[6,4,8,64,128]{4,3,2,1,0:T(8,128)(2,1)}, bf16[6,4,8,64,128]{4,3,2,1,0:T(8,128)(2,1)S(1)}, u32[]{:S(2)}) copy-start(bf16[6,4,8,64,128]{4,3,2,1,0:T(8,128)(2,1)S(1)} %bitcast_dynamic-update-slice_fusion.7) | copy-start | bytes 9437188
  8.3 2.3 %copy-start.24 = (f32[6,128,128]{2,1,0:T(8,128)S(1)}, f32[6,128,128]{2,1,0:T(8,128)}, u32[]{:S(2)}) copy-start(f32[6,128,128]{2,1,0:T(8,128)} %param.6) | copy-start | bytes 1179652
  8.9 1.7 copy-start.11
  17.0 2.7 %copy-start.3 = (f32[6,4,8,64,128]{4,3,2,1,0:T(8,128)}, f32[6,4,8,64,128]{4,3,2,1,0:T(8,128)S(1)}, u32[]{:S(2)}) copy-start(f32[6,4,8,64,128]{4,3,2,1,0:T(8,128)S(1)} %get-tuple-element.63) | copy-start | bytes 18874372
  19.7 5.9 %copy-start.8 = (bf16[6,4,8,64,128]{4,3,2,1,0:T(8,128)(2,1)}, bf16[6,4,8,64,128]{4,3,2,1,0:T(8,128)(2,1)S(1)}, u32[]{:S(2)}) copy-start(bf16[6,4,8,64,128]{4,3,2,1,0:T(8,128)(2,1)S(1)} %fusion.13) | copy-start | bytes 9437188
  20.4 24.8 %collective-permute-start = (bf16[1,8,64,128]{3,2,1,0:T(8,128)(2,1)}, bf16[1,8,64,128]{3,2,1,0:T(8,128)(2,1)}, u32[]{:S(2)}, u32[]{:S(2)}) collective-permute-start(bf16[1,8,64,128]{3,2,1,0:T(8,128)(2,1)} %get-tuple-element.21), channel_id=1, source_target_pairs={{0,8},{8,0},{16,24},{24,16},{32,40},{40,32},{48,56},{56,48},{64,72... | collective-permute-start | bytes 393224 | tf_op jit(solution)/shard_map/ppermute | solution.py:50
  23.6 21.6 %collective-permute-start.1 = (bf16[1,8,64,128]{3,2,1,0:T(8,128)(2,1)}, bf16[1,8,64,128]{3,2,1,0:T(8,128)(2,1)}, u32[]{:S(2)}, u32[]{:S(2)}) collective-permute-start(bf16[1,8,64,128]{3,2,1,0:T(8,128)(2,1)} %get-tuple-element.22), channel_id=1, source_target_pairs={{8,16},{16,8},{24,32},{32,24},{40,48},{48,40},{56,64},{64,56},{72,... | collective-permute-start | bytes 393224 | tf_op jit(solution)/shard_map/ppermute | solution.py:54
  25.8 7.8 %copy-start.22 = (bf16[4,8,64,128]{3,2,1,0:T(8,128)(2,1)}, bf16[4,8,64,128]{3,2,1,0:T(8,128)(2,1)S(1)}, u32[]{:S(2)}) copy-start(bf16[4,8,64,128]{3,2,1,0:T(8,128)(2,1)S(1)} %get-tuple-element.23) | copy-start | bytes 1572868
  25.8 14.1 %copy-start.20 = (bf16[4,8,64,128]{3,2,1,0:T(8,128)(2,1)}, bf16[4,8,64,128]{3,2,1,0:T(8,128)(2,1)S(1)}, u32[]{:S(2)}) copy-start(bf16[4,8,64,128]{3,2,1,0:T(8,128)(2,1)S(1)} %get-tuple-element.24) | copy-start | bytes 1572868
  25.8 14.0 %copy-start.23 = (bf16[4,8,64,128]{3,2,1,0:T(8,128)(2,1)}, bf16[4,8,64,128]{3,2,1,0:T(8,128)(2,1)S(1)}, u32[]{:S(2)}) copy-start(bf16[4,8,64,128]{3,2,1,0:T(8,128)(2,1)S(1)} %get-tuple-element.26) | copy-start | bytes 1572868
  26.6 17.8 %collective-permute-start.2 = (bf16[4,1,64,128]{3,2,1,0:T(8,128)(2,1)}, bf16[4,1,64,128]{3,2,1,0:T(8,128)(2,1)}, u32[]{:S(2)}, u32[]{:S(2)}) collective-permute-start(bf16[4,1,64,128]{3,2,1,0:T(8,128)(2,1)} %get-tuple-element.40), channel_id=1, source_target_pairs={{0,2},{2,0},{4,6},{6,4},{1,3},{3,1},{5,7},{7,5},{8,10},{10,8},{12,... | collective-permute-start | bytes 196616 | tf_op jit(solution)/shard_map/ppermute | solution.py:50
  27.2 17.1 %collective-permute-start.3 = (bf16[4,1,64,128]{3,2,1,0:T(8,128)(2,1)}, bf16[4,1,64,128]{3,2,1,0:T(8,128)(2,1)}, u32[]{:S(2)}, u32[]{:S(2)}) collective-permute-start(bf16[4,1,64,128]{3,2,1,0:T(8,128)(2,1)} %get-tuple-element.41), channel_id=1, source_target_pairs={{2,4},{4,2},{3,5},{5,3},{10,12},{12,10},{11,13},{13,11},{18,20},{2... | collective-permute-start | bytes 196616 | tf_op jit(solution)/shard_map/ppermute | solution.py:54
  29.2 15.2 %collective-permute-start.4 = (bf16[4,8,1,128]{3,2,1,0:T(2,128)(2,1)}, bf16[4,8,1,128]{3,2,1,0:T(2,128)(2,1)S(1)}, u32[]{:S(2)}, u32[]{:S(2)}) collective-permute-start(bf16[4,8,1,128]{3,2,1,0:T(2,128)(2,1)} %broadcast_select_fusion.27), channel_id=1, source_target_pairs={{0,1},{1,0},{2,3},{3,2},{4,5},{5,4},{6,7},{7,6},{8,9},{9,8},{10,11... | collective-permute-start | bytes 24584 | tf_op jit(solution)/shard_map/ppermute | solution.py:50
  39.8 6.5 %copy-start.10 = (bf16[4,8,64,128]{3,2,1,0:T(8,128)(2,1)S(1)}, bf16[4,8,64,128]{3,2,1,0:T(8,128)(2,1)}, u32[]{:S(2)}) copy-start(bf16[4,8,64,128]{3,2,1,0:T(8,128)(2,1)} %param.5) | copy-start | bytes 1572868
  48.6 14.4 %copy-start.15 = (f32[4,8,64,128]{3,2,1,0:T(8,128)}, f32[4,8,64,128]{3,2,1,0:T(8,128)S(1)}, u32[]{:S(2)}) copy-start(f32[4,8,64,128]{3,2,1,0:T(8,128)S(1)} %get-tuple-element.13) | copy-start | bytes 3145732
  48.6 14.3 %copy-start.16 = (bf16[4,7,64,128]{3,2,1,0:T(8,128)(2,1)S(1)}, bf16[4,7,64,128]{3,2,1,0:T(8,128)(2,1)}, u32[]{:S(2)}) copy-start(bf16[4,7,64,128]{3,2,1,0:T(8,128)(2,1)} %slice.286) | copy-start | bytes 1376260
  48.6 14.3 %copy-start.17 = (bf16[4,7,64,128]{3,2,1,0:T(8,128)(2,1)S(1)}, bf16[4,7,64,128]{3,2,1,0:T(8,128)(2,1)}, u32[]{:S(2)}) copy-start(bf16[4,7,64,128]{3,2,1,0:T(8,128)(2,1)} %slice.287) | copy-start | bytes 1376260
  48.6 14.3 %copy-start.18 = (bf16[3,8,64,128]{3,2,1,0:T(8,128)(2,1)S(1)}, bf16[3,8,64,128]{3,2,1,0:T(8,128)(2,1)}, u32[]{:S(2)}) copy-start(bf16[3,8,64,128]{3,2,1,0:T(8,128)(2,1)} %get-tuple-element.19) | copy-start | bytes 1179652
  48.6 14.3 %copy-start.19 = (bf16[3,8,64,128]{3,2,1,0:T(8,128)(2,1)S(1)}, bf16[3,8,64,128]{3,2,1,0:T(8,128)(2,1)}, u32[]{:S(2)}) copy-start(bf16[3,8,64,128]{3,2,1,0:T(8,128)(2,1)} %get-tuple-element.20) | copy-start | bytes 1179652
  63.0 14.8 %slice-start = ((s8[6291456]{0:T(1024)(128)(4,1)}), s8[4194304]{0:T(1024)(128)(4,1)S(1)}, s32[]{:S(2)}) async-start(s8[6291456]{0:T(1024)(128)(4,1)} %bitcast.355), calls=%async_computation.2 | async-start | bytes 8388608
  63.8 11.0 %collective-permute-start.9 = (bf16[4,8,1,128]{3,2,1,0:T(2,128)(2,1)S(1)}, bf16[4,8,1,128]{3,2,1,0:T(2,128)(2,1)S(1)}, u32[]{:S(2)}, u32[]{:S(2)}) collective-permute-start(bf16[4,8,1,128]{3,2,1,0:T(2,128)(2,1)S(1)} %broadcast_select_fusion.24), channel_id=1, source_target_pairs={{0,1},{1,0},{2,3},{3,2},{4,5},{5,4},{6,7},{7,6},{8,9},{9,8},{10,11... | collective-permute-start | bytes 24584 | tf_op jit(solution)/shard_map/ppermute | solution.py:50
  64.0 13.7 %slice-start.1 = ((s8[6291456]{0:T(1024)(128)(4,1)}), s8[2097152]{0:T(1024)(128)(4,1)S(1)}, s32[]{:S(2)}) async-start(s8[6291456]{0:T(1024)(128)(4,1)} %bitcast.355), calls=%async_computation.3 | async-start | bytes 4194304
  64.3 10.5 %collective-permute-start.7 = (bf16[4,1,64,128]{3,2,1,0:T(8,128)(2,1)S(1)}, bf16[4,1,64,128]{3,2,1,0:T(8,128)(2,1)S(1)}, u32[]{:S(2)}, u32[]{:S(2)}) collective-permute-start(bf16[4,1,64,128]{3,2,1,0:T(8,128)(2,1)S(1)} %get-tuple-element.37), channel_id=1, source_target_pairs={{2,4},{4,2},{3,5},{5,3},{10,12},{12,10},{11,13},{13,11},{18,20},{2... | collective-permute-start | bytes 196616 | tf_op jit(solution)/shard_map/ppermute | solution.py:54
  65.1 9.7 %collective-permute-start.8 = (bf16[4,1,64,128]{3,2,1,0:T(8,128)(2,1)S(1)}, bf16[4,1,64,128]{3,2,1,0:T(8,128)(2,1)S(1)}, u32[]{:S(2)}, u32[]{:S(2)}) collective-permute-start(bf16[4,1,64,128]{3,2,1,0:T(8,128)(2,1)S(1)} %get-tuple-element.36), channel_id=1, source_target_pairs={{0,2},{2,0},{4,6},{6,4},{1,3},{3,1},{5,7},{7,5},{8,10},{10,8},{12,... | collective-permute-start | bytes 196616 | tf_op jit(solution)/shard_map/ppermute | solution.py:50
  69.4 7.7 %collective-permute-start.5 = (bf16[1,8,64,128]{3,2,1,0:T(8,128)(2,1)S(1)}, bf16[1,8,64,128]{3,2,1,0:T(8,128)(2,1)S(1)}, u32[]{:S(2)}, u32[]{:S(2)}) collective-permute-start(bf16[1,8,64,128]{3,2,1,0:T(8,128)(2,1)S(1)} %get-tuple-element.39), channel_id=1, source_target_pairs={{8,16},{16,8},{24,32},{32,24},{40,48},{48,40},{56,64},{64,56},{72,... | collective-permute-start | bytes 393224 | tf_op jit(solution)/shard_map/ppermute | solution.py:54
  74.4 2.6 %collective-permute-start.6 = (bf16[1,8,64,128]{3,2,1,0:T(8,128)(2,1)S(1)}, bf16[1,8,64,128]{3,2,1,0:T(8,128)(2,1)S(1)}, u32[]{:S(2)}, u32[]{:S(2)}) collective-permute-start(bf16[1,8,64,128]{3,2,1,0:T(8,128)(2,1)S(1)} %get-tuple-element.38), channel_id=1, source_target_pairs={{0,8},{8,0},{16,24},{24,16},{32,40},{40,32},{48,56},{56,48},{64,72... | collective-permute-start | bytes 393224 | tf_op jit(solution)/shard_map/ppermute | solution.py:50
  77.7 3.8 %copy-start.14 = (bf16[6,4,8,64,128]{4,3,2,1,0:T(8,128)(2,1)S(1)}, bf16[6,4,8,64,128]{4,3,2,1,0:T(8,128)(2,1)}, u32[]{:S(2)}) copy-start(bf16[6,4,8,64,128]{4,3,2,1,0:T(8,128)(2,1)} %get-tuple-element.68) | copy-start | bytes 9437188
  77.8 3.8 %copy-start.27 = (f32[6,4,8,64]{3,2,1,0:T(8,128)S(1)}, f32[6,4,8,64]{3,2,1,0:T(8,128)}, u32[]{:S(2)}) copy-start(f32[6,4,8,64]{3,2,1,0:T(8,128)} %broadcast_divide_fusion.1) | copy-start | bytes 147460
  87.2 5.5 %copy-start.1 = (bf16[6,4,8,64,128]{4,3,2,1,0:T(8,128)(2,1)S(1)}, bf16[6,4,8,64,128]{4,3,2,1,0:T(8,128)(2,1)}, u32[]{:S(2)}) copy-start(bf16[6,4,8,64,128]{4,3,2,1,0:T(8,128)(2,1)} %param.8) | copy-start | bytes 9437188
  93.9 1.9 %copy-start.9 = (f32[4,8,64,128]{3,2,1,0:T(8,128)}, f32[4,8,64,128]{3,2,1,0:T(8,128)S(1)}, u32[]{:S(2)}) copy-start(f32[4,8,64,128]{3,2,1,0:T(8,128)S(1)} %get-tuple-element.5) | copy-start | bytes 3145732
  93.9 1.9 %copy-start.5 = (f32[4,8,64,128]{3,2,1,0:T(8,128)}, f32[4,8,64,128]{3,2,1,0:T(8,128)S(1)}, u32[]{:S(2)}) copy-start(f32[4,8,64,128]{3,2,1,0:T(8,128)S(1)} %get-tuple-element.7) | copy-start | bytes 3145732
  94.4 1.5 copy-start.6
  94.4 11.3 %collective-permute-start.14 = (bf16[4,8,1,128]{3,2,1,0:T(2,128)(2,1)S(1)}, bf16[4,8,1,128]{3,2,1,0:T(2,128)(2,1)S(1)}, u32[]{:S(2)}, u32[]{:S(2)}) collective-permute-start(bf16[4,8,1,128]{3,2,1,0:T(2,128)(2,1)S(1)} %broadcast_select_fusion.21), channel_id=1, source_target_pairs={{0,1},{1,0},{2,3},{3,2},{4,5},{5,4},{6,7},{7,6},{8,9},{9,8},{10,11... | collective-permute-start | bytes 24584 | tf_op jit(solution)/shard_map/ppermute | solution.py:50
  95.8 1.3 copy-start.21
  95.8 13.1 %slice-start.2 = ((s8[6291456]{0:T(1024)(128)(4,1)}), s8[2097152]{0:T(1024)(128)(4,1)S(1)}, s32[]{:S(2)}) async-start(s8[6291456]{0:T(1024)(128)(4,1)} %bitcast.357), calls=%async_computation.4 | async-start | bytes 4194304
  97.1 11.9 %slice-start.3 = ((s8[6291456]{0:T(1024)(128)(4,1)}), s8[4194304]{0:T(1024)(128)(4,1)S(1)}, s32[]{:S(2)}) async-start(s8[6291456]{0:T(1024)(128)(4,1)} %bitcast.357), calls=%async_computation.5 | async-start | bytes 8388608
  97.1 11.2 %slice-start.4 = ((bf16[4,8,64,128]{3,2,1,0:T(8,128)(2,1)}), bf16[3,8,64,128]{3,2,1,0:T(8,128)(2,1)S(1)}, s32[]{:S(2)}) async-start(bf16[4,8,64,128]{3,2,1,0:T(8,128)(2,1)} %copy-done.21), calls=%async_computation.6 | async-start | bytes 786432 | tf_op jit(solution)/shard_map/slice | solution.py:106
  97.4 8.4 %collective-permute-start.12 = (bf16[4,1,64,128]{3,2,1,0:T(8,128)(2,1)S(1)}, bf16[4,1,64,128]{3,2,1,0:T(8,128)(2,1)S(1)}, u32[]{:S(2)}, u32[]{:S(2)}) collective-permute-start(bf16[4,1,64,128]{3,2,1,0:T(8,128)(2,1)S(1)} %get-tuple-element.28), channel_id=1, source_target_pairs={{2,4},{4,2},{3,5},{5,3},{10,12},{12,10},{11,13},{13,11},{18,20},{2... | collective-permute-start | bytes 196616 | tf_op jit(solution)/shard_map/ppermute | solution.py:54
  98.2 7.6 %collective-permute-start.13 = (bf16[4,1,64,128]{3,2,1,0:T(8,128)(2,1)S(1)}, bf16[4,1,64,128]{3,2,1,0:T(8,128)(2,1)S(1)}, u32[]{:S(2)}, u32[]{:S(2)}) collective-permute-start(bf16[4,1,64,128]{3,2,1,0:T(8,128)(2,1)S(1)} %get-tuple-element.27), channel_id=1, source_target_pairs={{0,2},{2,0},{4,6},{6,4},{1,3},{3,1},{5,7},{7,5},{8,10},{10,8},{12,... | collective-permute-start | bytes 196616 | tf_op jit(solution)/shard_map/ppermute | solution.py:50
  101.2 7.1 %collective-permute-start.10 = (bf16[1,8,64,128]{3,2,1,0:T(8,128)(2,1)S(1)}, bf16[1,8,64,128]{3,2,1,0:T(8,128)(2,1)S(1)}, u32[]{:S(2)}, u32[]{:S(2)}) collective-permute-start(bf16[1,8,64,128]{3,2,1,0:T(8,128)(2,1)S(1)} %get-tuple-element.30), channel_id=1, source_target_pairs={{8,16},{16,8},{24,32},{32,24},{40,48},{48,40},{56,64},{64,56},{72,... | collective-permute-start | bytes 393224 | tf_op jit(solution)/shard_map/ppermute | solution.py:54
  105.6 2.6 %collective-permute-start.11 = (bf16[1,8,64,128]{3,2,1,0:T(8,128)(2,1)S(1)}, bf16[1,8,64,128]{3,2,1,0:T(8,128)(2,1)S(1)}, u32[]{:S(2)}, u32[]{:S(2)}) collective-permute-start(bf16[1,8,64,128]{3,2,1,0:T(8,128)(2,1)S(1)} %get-tuple-element.29), channel_id=1, source_target_pairs={{0,8},{8,0},{16,24},{24,16},{32,40},{40,32},{48,56},{56,48},{64,72... | collective-permute-start | bytes 393224 | tf_op jit(solution)/shard_map/ppermute | solution.py:50
  109.0 3.9 %copy-start.7 = (bf16[6,4,8,64,128]{4,3,2,1,0:T(8,128)(2,1)}, bf16[6,4,8,64,128]{4,3,2,1,0:T(8,128)(2,1)S(1)}, u32[]{:S(2)}) copy-start(bf16[6,4,8,64,128]{4,3,2,1,0:T(8,128)(2,1)S(1)} %fusion.66) | copy-start | bytes 9437188
  109.0 3.9 %copy-start.12 = (bf16[6,4,8,64,128]{4,3,2,1,0:T(8,128)(2,1)S(1)}, bf16[6,4,8,64,128]{4,3,2,1,0:T(8,128)(2,1)}, u32[]{:S(2)}) copy-start(bf16[6,4,8,64,128]{4,3,2,1,0:T(8,128)(2,1)} %get-tuple-element.67) | copy-start | bytes 9437188
  109.0 3.9 %copy-start.26 = (f32[6,4,8,64]{3,2,1,0:T(8,128)S(1)}, f32[6,4,8,64]{3,2,1,0:T(8,128)}, u32[]{:S(2)}) copy-start(f32[6,4,8,64]{3,2,1,0:T(8,128)} %broadcast_divide_fusion) | copy-start | bytes 147460
  119.2 39.3 %all-to-all-start = ((f32[256,1,384]{2,1,0:T(1,128)}), f32[256,1,384]{2,1,0:T(1,128)}, u32[]{:S(2)}, u32[]{:S(2)}) async-start(f32[256,1,384]{2,1,0:T(1,128)} %bitcast.75), calls=%async_computation | async-start | bytes 786432 | tf_op jit(solution)/shard_map/all_to_all | solution.py:166
  140.9 27.0 %copy-start.2 = (bf16[6,4,8,64,128]{4,3,2,1,0:T(8,128)(2,1)S(1)}, bf16[6,4,8,64,128]{4,3,2,1,0:T(8,128)(2,1)}, u32[]{:S(2)}) copy-start(bf16[6,4,8,64,128]{4,3,2,1,0:T(8,128)(2,1)} %param.8) | copy-start | bytes 9437188
  160.7 24.9 %all-to-all-start.1 = ((f32[256,1,384]{2,1,0:T(1,128)}), f32[256,1,384]{2,1,0:T(1,128)}, u32[]{:S(2)}, u32[]{:S(2)}) async-start(f32[256,1,384]{2,1,0:T(1,128)} %broadcast_in_dim.11), calls=%async_computation.1 | async-start | bytes 786432 | tf_op jit(solution)/shard_map/all_to_all | solution.py:168
  168.0 17.7 %copy-start.25 = (f32[6,128,128]{2,1,0:T(8,128)S(1)}, f32[6,128,128]{2,1,0:T(8,128)}, u32[]{:S(2)}) copy-start(f32[6,128,128]{2,1,0:T(8,128)} %param.6) | copy-start | bytes 1179652

commit v3 on v2

--- a/solution.py
+++ b/solution.py
@@ -158,13 +158,14 @@
     return (unary_term, grad_messages)
 
 
-def all_sum(value, axes):
+def all_sum(value, scale, axes):
     count = 1
     for axis in axes:
         count *= lax.axis_size(axis)
     rows = value.reshape(count, -1)
     mine = jnp.sum(lax.all_to_all(rows, axes, 0, 0, tiled=True), axis=0, keepdims=True)
-    spread_out = jnp.broadcast_to(mine, rows.shape)
+    own = lax.dynamic_slice_in_dim(scale.reshape(count, -1), lax.axis_index(axes), 1, axis=0)
+    spread_out = jnp.broadcast_to(own * mine, rows.shape)
     return lax.all_to_all(spread_out, axes, 0, 0, tiled=True).reshape(value.shape)
 
 
@@ -205,8 +206,7 @@
         total_one = total_one + ratios_one[index]
     grad_potential = grad_potential + whole_one * total_one
     grad_unary = potential * grad_potential
-    summed = all_sum(weights_two + weights_one, ("gx", "gy", "gz"))
-    grad_compat = weights * summed
+    grad_compat = all_sum(weights_two + weights_one, weights, ("gx", "gy", "gz"))
     return (grad_unary, grad_compat)
 
 

time: 188 us -> 186 us (0.989)
  local copies, waits for them, and re-layouts: 11.8 us -> 15.7 us
  other arithmetic: 56.9 us -> 54.5 us
  matrix products: 34.8 us -> 32.9 us
    another operation x1, other arithmetic: 2.56 us -> 0.44 us  [send_terms(): hidden_b = jnp.stack(hidden).astype(jnp.bfloat16)]
    dot_general x2, matrix products: 10.1 us -> 8.15 us  [send_terms(): jnp.einsum('dxyzk,dkl->dxyzl', hidden_b, weights_b, preferred_element_typ...]
    unnamed x64 -> x65, local copies, waits for them, and re-layouts: 4.22 us -> 5.67 us
  transfers between devices with their start and end apart: 17 -> 17, of which waited for: 4 -> 4; matrix products, arithmetic and copies ran while one was open for 18% -> 19% of each run, Pallas kernels for 0% -> 0%
where the time goes in v3:
time: 186 us; the launch traced here: 185 us
  starting transfers between devices  55.5 us (30%)
  other arithmetic  54.5 us (29%)
  matrix products  32.9 us (18%)
  waiting for transfers between devices  25.1 us (13%)
  local copies, waits for them, and re-layouts  15.7 us (8%)
    all_to_all x1, starting transfers between devices, all_sum(): lax.all_to_all(rows, axes, 0, 0, tiled=True)  21.8 us
    sub x1, other arithmetic, belief_adjoint(): cotangent - jnp.sum(cotangent * belief, axis=-1, keepdims=True)  14.3 us
    ppermute x6, starting transfers between devices, trade(): lax.ppermute(jnp.where(odd, high_face, low_face), axis, [(i, i + 1 if i %...  14.3 us
    ppermute x9, starting transfers between devices, trade(): lax.ppermute(jnp.where(odd, low_face, high_face), axis, [(i, i ^ 1) for i...  13.7 us
    dot_general x2, matrix products, local_adjoint(): jnp.einsum('dxyzl,dkl->dxyzk', grad_out, weights_b, preferred_element_typ...  12.8 us
    dot_general x2, matrix products, local_adjoint(): jnp.einsum('dxyzk,dxyzl->dkl', hidden_b, grad_out, preferred_element_type...  11.9 us
    all_to_all x1, waiting for transfers between devices, all_sum(): lax.all_to_all(spread_out, axes, 0, 0, tiled=True).reshape(value.shape)  11.1 us
    all_to_all x1, waiting for transfers between devices, all_sum(): lax.all_to_all(rows, axes, 0, 0, tiled=True)  9.25 us
  transfers between devices with their start and end apart: 17, of which 4 were waited for; matrix products, arithmetic and copies ran while one was open for 19% of the time, Pallas kernels for 0%

profile of v3, /device:TPU:1, one launch (start us, length us, event | category | flops | bytes accessed | tf_op | source)
XLA Modules:
  0.0 185.4 jit_solution(8429799644347650207)
XLA Ops:
  0.7 4.7 %bitcast_dynamic-update-slice_fusion.5 = (bf16[6,4,8,64,128]{4,3,2,1,0:T(8,128)(2,1)S(1)}, f32[4,8,64,128]{3,2,1,0:T(8,128)S(1)}, bf16[6,4,8,64,128]{4,3,2,1,0:T(8,128)(2,1)S(1)}, f32[4,8,64,128]{3,2,1,0:T(8,128)S(1)}) fusion(bf16[6,4,8,64,128]{4,3,2,1,0:T(8,128)(2,1)} %param.7, bf16[4,8,64,128]{3,2,1,0:T(8,128)(2,1)} %param.5, ...), kind=kLoop, calls=%fused_computation.152 | loop fusion | flops 7602174 | bytes 9961472
  6.3 1.2 copy-done.4
  7.7 0.2 bitcast_dynamic-update-slice_fusion.3
  8.0 0.2 bitcast_dynamic-update-slice_fusion.2
  8.4 0.3 copy-done.27
  8.7 0.8 fusion.84
  9.5 0.4 bitcast_dynamic-update-slice_fusion
  10.0 1.6 copy-done.11
  11.6 1.9 %fusion.85 = (f32[6,4,8,64]{3,2,1,0:T(8,128)S(1)}, f32[6,4,8,64,128]{4,3,2,1,0:T(8,128)S(1)}) fusion(bf16[6,4,8,64,128]{4,3,2,1,0:T(8,128)(2,1)S(1)} %get-tuple-element.70, bf16[6,128,128]{2,1,0:T(8,128)(2,1)S(1)} %get-tuple-element.45), kind=kOutput, calls=%fused_computation.216 | convolution fusion | flops 404213760 | bytes 9682944 | tf_op jit(solution)/shard_map/dxyzk,dkl->dxyzl/dot_general | solution.py:38
  13.5 2.0 %fusion.13 = bf16[6,4,8,64,128]{4,3,2,1,0:T(8,128)(2,1)S(1)} fusion(f32[6,4,8,64]{3,2,1,0:T(8,128)S(1)} %get-tuple-element.64, f32[6,4,8,64,128]{4,3,2,1,0:T(8,128)S(1)} %get-tuple-element.65), kind=kLoop, calls=%fused_computation.18 | loop fusion | flops 4718592 | bytes 9486336 | tf_op jit(solution)/shard_map/convert.29
  15.5 0.6 copy-done.3
  16.2 0.8 select_bitcast_fusion.1
  17.0 1.0 copy-done.8
  18.0 3.2 %collective-permute-start = (bf16[1,8,64,128]{3,2,1,0:T(8,128)(2,1)}, bf16[1,8,64,128]{3,2,1,0:T(8,128)(2,1)}, u32[]{:S(2)}, u32[]{:S(2)}) collective-permute-start(bf16[1,8,64,128]{3,2,1,0:T(8,128)(2,1)} %get-tuple-element.21), channel_id=1, source_target_pairs={{0,8},{8,0},{16,24},{24,16},{32,40},{40,32},{48,56},{56,48},{64,72... | collective-permute-start | bytes 393224 | tf_op jit(solution)/shard_map/ppermute | solution.py:50
  21.2 1.9 %collective-permute-start.1 = (bf16[1,8,64,128]{3,2,1,0:T(8,128)(2,1)}, bf16[1,8,64,128]{3,2,1,0:T(8,128)(2,1)}, u32[]{:S(2)}, u32[]{:S(2)}) collective-permute-start(bf16[1,8,64,128]{3,2,1,0:T(8,128)(2,1)} %get-tuple-element.22), channel_id=1, source_target_pairs={{8,16},{16,8},{24,32},{32,24},{40,48},{48,40},{56,64},{64,56},{72,... | collective-permute-start | bytes 393224 | tf_op jit(solution)/shard_map/ppermute | solution.py:54
  23.1 1.8 slice_bitcast_fusion.15
  24.9 0.7 broadcast_select_fusion.17
  25.7 0.7 collective-permute-start.2
  26.3 1.3 collective-permute-start.3
  27.6 0.6 broadcast_select_fusion.27
  28.2 1.6 collective-permute-start.4
  29.9 2.1 %slice_bitcast_fusion.17 = (bf16[3,8,64,128]{3,2,1,0:T(8,128)(2,1)}, bf16[3,8,64,128]{3,2,1,0:T(8,128)(2,1)}) fusion(bf16[6,4,8,64,128]{4,3,2,1,0:T(8,128)(2,1)} %copy-done.8), kind=kLoop, calls=%fused_computation.161 | loop fusion | bytes 1572864 | tf_op jit(solution)/shard_map/slice | solution.py:82
  32.0 0.7 broadcast_divide_fusion.1
  32.6 6.3 %fusion.86 = (f32[6,4,8,64]{3,2,1,0:T(8,128)S(1)}, f32[6,4,8,64,128]{4,3,2,1,0:T(8,128)}) fusion(bf16[6,4,8,64,128]{4,3,2,1,0:T(8,128)(2,1)} %copy-done.11, bf16[6,128,128]{2,1,0:T(8,128)(2,1)S(1)} %get-tuple-element.45), kind=kOutput, calls=%fused_computation.217 | convolution fusion | flops 404213760 | bytes 9682944 | tf_op jit(solution)/shard_map/dxyzk,dkl->dxyzl/dot_general | solution.py:38
  38.9 0.7 broadcast_divide_fusion
  39.8 1.8 slice.286
  41.6 1.8 slice.287
  43.5 0.9 select_select_fusion.3
  44.4 1.0 select_select_fusion.1
  45.4 2.3 %fusion.79 = (f32[4,8,64]{2,1,0:T(8,128)S(1)}, f32[4,8,64,128]{3,2,1,0:T(8,128)S(1)}) fusion(bf16[4,8,64,128]{3,2,1,0:T(8,128)(2,1)S(1)} %copy-done.10, bf16[4,8,1,128]{3,2,1,0:T(2,128)(2,1)S(1)} %get-tuple-element.62, bf16[4,8,63,128]{3,2,1,0:T(8,128)(2,1)S(1)} %slice.293, bf16[4,8,63,128]{3,2,1,0:T(8,128)(2,1)} %bitcast.367, ...), kind=kLoop, calls=%fused_computation.214 | loop fusion | flops 8386560 | bytes 4726784 | tf_op jit(solution)/shard_map/reduce_sum | solution.py:121
  47.7 14.3 %fusion.36 = (bf16[4,8,64,128]{3,2,1,0:T(8,128)(2,1)S(1)}, f32[4,8,64,128]{3,2,1,0:T(8,128)S(1)}, f32[4,8,64,128]{3,2,1,0:T(8,128)}) fusion(bf16[4,8,63,128]{3,2,1,0:T(8,128)(2,1)} %bitcast.368, bf16[4,8,1,128]{3,2,1,0:T(2,128)(2,1)S(1)} %get-tuple-element.63, f32[4,8,64,128]{3,2,1,0:T(8,128)S(1)} %get-tuple-element.13, ...), kind=kOutput, calls=%fused_computation.74 | output fusion | flops 4196479 | bytes 5775360 | tf_op jit(solution)/shard_map/sub | solution.py:123
  62.1 0.7 fusion.37
  63.4 0.8 collective-permute-start.7
  64.2 4.3 %collective-permute-start.8 = (bf16[4,1,64,128]{3,2,1,0:T(8,128)(2,1)S(1)}, bf16[4,1,64,128]{3,2,1,0:T(8,128)(2,1)S(1)}, u32[]{:S(2)}, u32[]{:S(2)}) collective-permute-start(bf16[4,1,64,128]{3,2,1,0:T(8,128)(2,1)S(1)} %get-tuple-element.36), channel_id=1, source_target_pairs={{0,2},{2,0},{4,6},{6,4},{1,3},{3,1},{5,7},{7,5},{8,10},{10,8},{12,... | collective-permute-start | bytes 196616 | tf_op jit(solution)/shard_map/ppermute | solution.py:50
  68.5 5.1 %collective-permute-start.5 = (bf16[1,8,64,128]{3,2,1,0:T(8,128)(2,1)S(1)}, bf16[1,8,64,128]{3,2,1,0:T(8,128)(2,1)S(1)}, u32[]{:S(2)}, u32[]{:S(2)}) collective-permute-start(bf16[1,8,64,128]{3,2,1,0:T(8,128)(2,1)S(1)} %get-tuple-element.39), channel_id=1, source_target_pairs={{8,16},{16,8},{24,32},{32,24},{40,48},{48,40},{56,64},{64,56},{72,... | collective-permute-start | bytes 393224 | tf_op jit(solution)/shard_map/ppermute | solution.py:54
  73.5 0.3 collective-permute-start.6
  73.9 2.2 %collective-permute-done.5 = bf16[1,8,64,128]{3,2,1,0:T(8,128)(2,1)S(1)} collective-permute-done((bf16[1,8,64,128]{3,2,1,0:T(8,128)(2,1)S(1)}, bf16[1,8,64,128]{3,2,1,0:T(8,128)(2,1)S(1)}, u32[]{:S(2)}, u32[]{:S(2)}) %collective-permute-start.5) | collective-permute-done | bytes 131104 | tf_op jit(solution)/shard_map/ppermute | solution.py:54
  76.6 0.2 fusion.60
  76.9 3.8 %fusion.1 = f32[6,4,8,64]{3,2,1,0:T(8,128)S(1)} fusion(bf16[6,4,8,64,128]{4,3,2,1,0:T(8,128)(2,1)S(1)} %fusion.60, f32[6,4,8,64]{3,2,1,0:T(8,128)S(1)} %get-tuple-element.64, f32[6,4,8,64,128]{4,3,2,1,0:T(8,128)S(1)} %bitcast.363), kind=kLoop, calls=%fused_computation.5 | loop fusion | flops 7852032 | bytes 9535488 | tf_op jit(solution)/shard_map/reduce_sum | solution.py:132
  80.7 5.7 %fusion.17 = f32[6,128,128]{2,1,0:T(8,128)S(1)} fusion(bf16[6,4,8,64,128]{4,3,2,1,0:T(8,128)(2,1)S(1)} %copy-done.14, bf16[6,4,8,64,128]{4,3,2,1,0:T(8,128)(2,1)S(1)} %fusion.60, f32[6,4,8,64]{3,2,1,0:T(8,128)S(1)} %broadcast_multiply_fusion.1, f32[6,4,8,64]{3,2,1,0:T(8,128)S(1)} %copy-done.26), kind=kOutput, calls=%fused_computation.67 | convolution fusion | flops 408944640 | bytes 6782976 | tf_op jit(solution)/shard_map/dxyzk,dxyzl->dkl/dot_general | solution.py:134
  86.3 5.5 %fusion.72 = f32[6,4,8,64,128]{4,3,2,1,0:T(8,128)S(1)} fusion(bf16[6,128,128]{2,1,0:T(8,128)(2,1)S(1)} %get-tuple-element.45, bf16[6,4,8,64,128]{4,3,2,1,0:T(8,128)(2,1)S(1)} %fusion.60, f32[6,4,8,64]{3,2,1,0:T(8,128)S(1)} %broadcast_multiply_fusion.1, f32[6,4,8,64]{3,2,1,0:T(8,128)S(1)} %copy-done.26), kind=kOutput, calls=%fused_computation.167 | convolution fusion | flops 408944640 | bytes 9732096 | tf_op jit(solution)/shard_map/dxyzl,dkl->dxyzk/dot_general | solution.py:137
  91.9 1.1 multiply_convert_fusion.1
  93.0 0.5 multiply_convert_fusion
  93.5 0.4 collective-permute-start.14
  93.9 1.0 multiply_convert_fusion.5
  94.9 1.2 multiply_convert_fusion.2
  96.5 0.8 collective-permute-start.12
  97.3 2.9 %collective-permute-start.13 = (bf16[4,1,64,128]{3,2,1,0:T(8,128)(2,1)S(1)}, bf16[4,1,64,128]{3,2,1,0:T(8,128)(2,1)S(1)}, u32[]{:S(2)}, u32[]{:S(2)}) collective-permute-start(bf16[4,1,64,128]{3,2,1,0:T(8,128)(2,1)S(1)} %get-tuple-element.27), channel_id=1, source_target_pairs={{0,2},{2,0},{4,6},{6,4},{1,3},{3,1},{5,7},{7,5},{8,10},{10,8},{12,... | collective-permute-start | bytes 196616 | tf_op jit(solution)/shard_map/ppermute | solution.py:50
  100.3 4.5 %collective-permute-start.10 = (bf16[1,8,64,128]{3,2,1,0:T(8,128)(2,1)S(1)}, bf16[1,8,64,128]{3,2,1,0:T(8,128)(2,1)S(1)}, u32[]{:S(2)}, u32[]{:S(2)}) collective-permute-start(bf16[1,8,64,128]{3,2,1,0:T(8,128)(2,1)S(1)} %get-tuple-element.30), channel_id=1, source_target_pairs={{8,16},{16,8},{24,32},{32,24},{40,48},{48,40},{56,64},{64,56},{72,... | collective-permute-start | bytes 393224 | tf_op jit(solution)/shard_map/ppermute | solution.py:54
  104.9 2.4 %collective-permute-done.10 = bf16[1,8,64,128]{3,2,1,0:T(8,128)(2,1)S(1)} collective-permute-done((bf16[1,8,64,128]{3,2,1,0:T(8,128)(2,1)S(1)}, bf16[1,8,64,128]{3,2,1,0:T(8,128)(2,1)S(1)}, u32[]{:S(2)}, u32[]{:S(2)}) %collective-permute-start.10) | collective-permute-done | bytes 131104 | tf_op jit(solution)/shard_map/ppermute | solution.py:54
  107.8 0.2 fusion.66
  108.1 3.8 %fusion.4 = f32[6,4,8,64]{3,2,1,0:T(8,128)S(1)} fusion(bf16[6,4,8,64,128]{4,3,2,1,0:T(8,128)(2,1)S(1)} %fusion.66, f32[6,4,8,64,128]{4,3,2,1,0:T(8,128)S(1)} %bitcast.365, f32[6,4,8,64]{3,2,1,0:T(8,128)S(1)} %get-tuple-element.67), kind=kLoop, calls=%fused_computation.8 | loop fusion | flops 7852032 | bytes 9535488 | tf_op jit(solution)/shard_map/reduce_sum | solution.py:132
  112.0 6.3 %fusion.27 = f32[6,128,128]{2,1,0:T(8,128)} fusion(f32[6,128,128]{2,1,0:T(8,128)S(1)} %fusion.17, bf16[6,4,8,64,128]{4,3,2,1,0:T(8,128)(2,1)S(1)} %copy-done.12, bf16[6,4,8,64,128]{4,3,2,1,0:T(8,128)(2,1)S(1)} %fusion.66, f32[6,4,8,64]{3,2,1,0:T(8,128)S(1)} %broadcast_multiply_fusion, f32[6,4,8,64]{3,2,1,0:T(8,128)S(1)} %copy-done.25), kind=kOutput, calls=%fused_computation.69 | convolution fusion | flops 409042944 | bytes 7176192 | tf_op jit(solution)/shard_map/dxyzk,dxyzl->dkl/dot_general | solution.py:134
  118.2 21.8 %all-to-all-start = ((f32[256,1,384]{2,1,0:T(1,128)}), f32[256,1,384]{2,1,0:T(1,128)}, u32[]{:S(2)}, u32[]{:S(2)}) async-start(f32[256,1,384]{2,1,0:T(1,128)} %bitcast.75), calls=%async_computation | async-start | bytes 786432 | tf_op jit(solution)/shard_map/all_to_all | solution.py:166
  140.1 0.8 reshape.79
  140.9 7.3 %fusion.68 = f32[6,4,8,64,128]{4,3,2,1,0:T(8,128)} fusion(bf16[6,128,128]{2,1,0:T(8,128)(2,1)S(1)} %get-tuple-element.45, bf16[6,4,8,64,128]{4,3,2,1,0:T(8,128)(2,1)} %copy-done.7, f32[6,4,8,64]{3,2,1,0:T(8,128)S(1)} %broadcast_multiply_fusion, f32[6,4,8,64]{3,2,1,0:T(8,128)S(1)} %copy-done.25), kind=kOutput, calls=%fused_computation.163 | convolution fusion | flops 408944640 | bytes 9732096 | tf_op jit(solution)/shard_map/dxyzl,dkl->dxyzk/dot_general | solution.py:137
  148.2 9.2 %all-to-all-done = f32[256,1,384]{2,1,0:T(1,128)} async-done(((f32[256,1,384]{2,1,0:T(1,128)}), f32[256,1,384]{2,1,0:T(1,128)}, u32[]{:S(2)}, u32[]{:S(2)}) %all-to-all-start) | async-done | bytes 393248 | tf_op jit(solution)/shard_map/all_to_all | solution.py:166
  157.5 1.3 reduce_sum.69
  158.8 0.7 multiply_reduce_fusion
  159.5 1.0 broadcast_in_dim.27
  160.4 5.7 %all-to-all-start.1 = ((f32[256,1,384]{2,1,0:T(1,128)}), f32[256,1,384]{2,1,0:T(1,128)S(1)}, u32[]{:S(2)}, u32[]{:S(2)}) async-start(f32[256,1,384]{2,1,0:T(1,128)} %broadcast_in_dim.27), calls=%async_computation.1 | async-start | bytes 786432 | tf_op jit(solution)/shard_map/all_to_all | solution.py:169
  166.2 7.3 %fusion.46 = f32[4,8,64,128]{3,2,1,0:T(8,128)} fusion(f32[6,4,8,64,128]{4,3,2,1,0:T(8,128)} %fusion.68, f32[4,8,64,128]{3,2,1,0:T(8,128)} %copy-done.5, f32[4,8,64,128]{3,2,1,0:T(8,128)} %get-tuple-element.66, f32[4,8,64,128]{3,2,1,0:T(8,128)} %copy-done.15, bf16[4,8,64,128]{3,2,1,0:T(8,128)(2,1)} %param.5, f32[4,8,64,128]{3,2,1,0:T(8,128)} %copy-done.9, ...), kind=kLoop, calls=%fused_computation.84 | loop fusion | flops 11010048 | bytes 19398656 | tf_op jit(solution)/shard_map/mul | solution.py:208
  173.5 11.1 %all-to-all-done.1 = f32[256,1,384]{2,1,0:T(1,128)S(1)} async-done(((f32[256,1,384]{2,1,0:T(1,128)}), f32[256,1,384]{2,1,0:T(1,128)S(1)}, u32[]{:S(2)}, u32[]{:S(2)}) %all-to-all-start.1) | async-done | bytes 393248 | tf_op jit(solution)/shard_map/all_to_all | solution.py:169
  184.7 0.7 copy.56
  (119 shorter events, 3.5 us)
Async XLA Ops:
  0.6 4.7 %copy-start = (bf16[6,4,8,64,128]{4,3,2,1,0:T(8,128)(2,1)S(1)}, bf16[6,4,8,64,128]{4,3,2,1,0:T(8,128)(2,1)}, u32[]{:S(2)}) copy-start(bf16[6,4,8,64,128]{4,3,2,1,0:T(8,128)(2,1)} %param.8) | copy-start | bytes 9437188
  5.6 1.9 %copy-start.4 = (bf16[6,4,8,64,128]{4,3,2,1,0:T(8,128)(2,1)S(1)}, bf16[6,4,8,64,128]{4,3,2,1,0:T(8,128)(2,1)}, u32[]{:S(2)}) copy-start(bf16[6,4,8,64,128]{4,3,2,1,0:T(8,128)(2,1)} %param.7) | copy-start | bytes 9437188
  7.7 1.0 copy-start.27
  10.0 1.7 copy-start.11
  10.0 3.5 %copy-start.13 = (bf16[6,4,8,64,128]{4,3,2,1,0:T(8,128)(2,1)}, bf16[6,4,8,64,128]{4,3,2,1,0:T(8,128)(2,1)S(1)}, u32[]{:S(2)}) copy-start(bf16[6,4,8,64,128]{4,3,2,1,0:T(8,128)(2,1)S(1)} %get-tuple-element.70) | copy-start | bytes 9437188
  13.5 2.7 %copy-start.3 = (f32[6,4,8,64,128]{4,3,2,1,0:T(8,128)}, f32[6,4,8,64,128]{4,3,2,1,0:T(8,128)S(1)}, u32[]{:S(2)}) copy-start(f32[6,4,8,64,128]{4,3,2,1,0:T(8,128)S(1)} %get-tuple-element.65) | copy-start | bytes 18874372
  16.2 1.8 copy-start.8
  18.0 26.4 %collective-permute-start = (bf16[1,8,64,128]{3,2,1,0:T(8,128)(2,1)}, bf16[1,8,64,128]{3,2,1,0:T(8,128)(2,1)}, u32[]{:S(2)}, u32[]{:S(2)}) collective-permute-start(bf16[1,8,64,128]{3,2,1,0:T(8,128)(2,1)} %get-tuple-element.21), channel_id=1, source_target_pairs={{0,8},{8,0},{16,24},{24,16},{32,40},{40,32},{48,56},{56,48},{64,72... | collective-permute-start | bytes 393224 | tf_op jit(solution)/shard_map/ppermute | solution.py:50
  21.2 23.2 %collective-permute-start.1 = (bf16[1,8,64,128]{3,2,1,0:T(8,128)(2,1)}, bf16[1,8,64,128]{3,2,1,0:T(8,128)(2,1)}, u32[]{:S(2)}, u32[]{:S(2)}) collective-permute-start(bf16[1,8,64,128]{3,2,1,0:T(8,128)(2,1)} %get-tuple-element.22), channel_id=1, source_target_pairs={{8,16},{16,8},{24,32},{32,24},{40,48},{48,40},{56,64},{64,56},{72,... | collective-permute-start | bytes 393224 | tf_op jit(solution)/shard_map/ppermute | solution.py:54
  24.9 7.7 %copy-start.22 = (bf16[4,8,64,128]{3,2,1,0:T(8,128)(2,1)}, bf16[4,8,64,128]{3,2,1,0:T(8,128)(2,1)S(1)}, u32[]{:S(2)}) copy-start(bf16[4,8,64,128]{3,2,1,0:T(8,128)(2,1)S(1)} %get-tuple-element.23) | copy-start | bytes 1572868
  24.9 14.0 %copy-start.20 = (bf16[4,8,64,128]{3,2,1,0:T(8,128)(2,1)}, bf16[4,8,64,128]{3,2,1,0:T(8,128)(2,1)S(1)}, u32[]{:S(2)}) copy-start(bf16[4,8,64,128]{3,2,1,0:T(8,128)(2,1)S(1)} %get-tuple-element.24) | copy-start | bytes 1572868
  24.9 14.0 %copy-start.23 = (bf16[4,8,64,128]{3,2,1,0:T(8,128)(2,1)}, bf16[4,8,64,128]{3,2,1,0:T(8,128)(2,1)S(1)}, u32[]{:S(2)}) copy-start(bf16[4,8,64,128]{3,2,1,0:T(8,128)(2,1)S(1)} %get-tuple-element.26) | copy-start | bytes 1572868
  25.7 17.8 %collective-permute-start.2 = (bf16[4,1,64,128]{3,2,1,0:T(8,128)(2,1)}, bf16[4,1,64,128]{3,2,1,0:T(8,128)(2,1)}, u32[]{:S(2)}, u32[]{:S(2)}) collective-permute-start(bf16[4,1,64,128]{3,2,1,0:T(8,128)(2,1)} %get-tuple-element.40), channel_id=1, source_target_pairs={{0,2},{2,0},{4,6},{6,4},{1,3},{3,1},{5,7},{7,5},{8,10},{10,8},{12,... | collective-permute-start | bytes 196616 | tf_op jit(solution)/shard_map/ppermute | solution.py:50
  26.3 17.1 %collective-permute-start.3 = (bf16[4,1,64,128]{3,2,1,0:T(8,128)(2,1)}, bf16[4,1,64,128]{3,2,1,0:T(8,128)(2,1)}, u32[]{:S(2)}, u32[]{:S(2)}) collective-permute-start(bf16[4,1,64,128]{3,2,1,0:T(8,128)(2,1)} %get-tuple-element.41), channel_id=1, source_target_pairs={{2,4},{4,2},{3,5},{5,3},{10,12},{12,10},{11,13},{13,11},{18,20},{2... | collective-permute-start | bytes 196616 | tf_op jit(solution)/shard_map/ppermute | solution.py:54
  28.2 15.2 %collective-permute-start.4 = (bf16[4,8,1,128]{3,2,1,0:T(2,128)(2,1)}, bf16[4,8,1,128]{3,2,1,0:T(2,128)(2,1)S(1)}, u32[]{:S(2)}, u32[]{:S(2)}) collective-permute-start(bf16[4,8,1,128]{3,2,1,0:T(2,128)(2,1)} %broadcast_select_fusion.27), channel_id=1, source_target_pairs={{0,1},{1,0},{2,3},{3,2},{4,5},{5,4},{6,7},{7,6},{8,9},{9,8},{10,11... | collective-permute-start | bytes 24584 | tf_op jit(solution)/shard_map/ppermute | solution.py:50
  38.9 6.5 %copy-start.10 = (bf16[4,8,64,128]{3,2,1,0:T(8,128)(2,1)S(1)}, bf16[4,8,64,128]{3,2,1,0:T(8,128)(2,1)}, u32[]{:S(2)}) copy-start(bf16[4,8,64,128]{3,2,1,0:T(8,128)(2,1)} %param.5) | copy-start | bytes 1572868
  47.7 14.4 %copy-start.15 = (f32[4,8,64,128]{3,2,1,0:T(8,128)}, f32[4,8,64,128]{3,2,1,0:T(8,128)S(1)}, u32[]{:S(2)}) copy-start(f32[4,8,64,128]{3,2,1,0:T(8,128)S(1)} %get-tuple-element.13) | copy-start | bytes 3145732
  47.7 14.3 %copy-start.16 = (bf16[4,7,64,128]{3,2,1,0:T(8,128)(2,1)S(1)}, bf16[4,7,64,128]{3,2,1,0:T(8,128)(2,1)}, u32[]{:S(2)}) copy-start(bf16[4,7,64,128]{3,2,1,0:T(8,128)(2,1)} %slice.286) | copy-start | bytes 1376260
  47.7 14.3 %copy-start.17 = (bf16[4,7,64,128]{3,2,1,0:T(8,128)(2,1)S(1)}, bf16[4,7,64,128]{3,2,1,0:T(8,128)(2,1)}, u32[]{:S(2)}) copy-start(bf16[4,7,64,128]{3,2,1,0:T(8,128)(2,1)} %slice.287) | copy-start | bytes 1376260
  47.7 14.3 %copy-start.18 = (bf16[3,8,64,128]{3,2,1,0:T(8,128)(2,1)S(1)}, bf16[3,8,64,128]{3,2,1,0:T(8,128)(2,1)}, u32[]{:S(2)}) copy-start(bf16[3,8,64,128]{3,2,1,0:T(8,128)(2,1)} %get-tuple-element.19) | copy-start | bytes 1179652
  47.7 14.3 %copy-start.19 = (bf16[3,8,64,128]{3,2,1,0:T(8,128)(2,1)S(1)}, bf16[3,8,64,128]{3,2,1,0:T(8,128)(2,1)}, u32[]{:S(2)}) copy-start(bf16[3,8,64,128]{3,2,1,0:T(8,128)(2,1)} %get-tuple-element.20) | copy-start | bytes 1179652
  62.1 14.8 %slice-start = ((s8[6291456]{0:T(1024)(128)(4,1)}), s8[4194304]{0:T(1024)(128)(4,1)S(1)}, s32[]{:S(2)}) async-start(s8[6291456]{0:T(1024)(128)(4,1)} %bitcast.362), calls=%async_computation.2 | async-start | bytes 8388608
  62.9 11.0 %collective-permute-start.9 = (bf16[4,8,1,128]{3,2,1,0:T(2,128)(2,1)S(1)}, bf16[4,8,1,128]{3,2,1,0:T(2,128)(2,1)S(1)}, u32[]{:S(2)}, u32[]{:S(2)}) collective-permute-start(bf16[4,8,1,128]{3,2,1,0:T(2,128)(2,1)S(1)} %broadcast_select_fusion.24), channel_id=1, source_target_pairs={{0,1},{1,0},{2,3},{3,2},{4,5},{5,4},{6,7},{7,6},{8,9},{9,8},{10,11... | collective-permute-start | bytes 24584 | tf_op jit(solution)/shard_map/ppermute | solution.py:50
  63.1 13.7 %slice-start.1 = ((s8[6291456]{0:T(1024)(128)(4,1)}), s8[2097152]{0:T(1024)(128)(4,1)S(1)}, s32[]{:S(2)}) async-start(s8[6291456]{0:T(1024)(128)(4,1)} %bitcast.362), calls=%async_computation.3 | async-start | bytes 4194304
  63.4 10.5 %collective-permute-start.7 = (bf16[4,1,64,128]{3,2,1,0:T(8,128)(2,1)S(1)}, bf16[4,1,64,128]{3,2,1,0:T(8,128)(2,1)S(1)}, u32[]{:S(2)}, u32[]{:S(2)}) collective-permute-start(bf16[4,1,64,128]{3,2,1,0:T(8,128)(2,1)S(1)} %get-tuple-element.37), channel_id=1, source_target_pairs={{2,4},{4,2},{3,5},{5,3},{10,12},{12,10},{11,13},{13,11},{18,20},{2... | collective-permute-start | bytes 196616 | tf_op jit(solution)/shard_map/ppermute | solution.py:54
  64.2 9.7 %collective-permute-start.8 = (bf16[4,1,64,128]{3,2,1,0:T(8,128)(2,1)S(1)}, bf16[4,1,64,128]{3,2,1,0:T(8,128)(2,1)S(1)}, u32[]{:S(2)}, u32[]{:S(2)}) collective-permute-start(bf16[4,1,64,128]{3,2,1,0:T(8,128)(2,1)S(1)} %get-tuple-element.36), channel_id=1, source_target_pairs={{0,2},{2,0},{4,6},{6,4},{1,3},{3,1},{5,7},{7,5},{8,10},{10,8},{12,... | collective-permute-start | bytes 196616 | tf_op jit(solution)/shard_map/ppermute | solution.py:50
  68.5 7.7 %collective-permute-start.5 = (bf16[1,8,64,128]{3,2,1,0:T(8,128)(2,1)S(1)}, bf16[1,8,64,128]{3,2,1,0:T(8,128)(2,1)S(1)}, u32[]{:S(2)}, u32[]{:S(2)}) collective-permute-start(bf16[1,8,64,128]{3,2,1,0:T(8,128)(2,1)S(1)} %get-tuple-element.39), channel_id=1, source_target_pairs={{8,16},{16,8},{24,32},{32,24},{40,48},{48,40},{56,64},{64,56},{72,... | collective-permute-start | bytes 393224 | tf_op jit(solution)/shard_map/ppermute | solution.py:54
  73.5 2.6 %collective-permute-start.6 = (bf16[1,8,64,128]{3,2,1,0:T(8,128)(2,1)S(1)}, bf16[1,8,64,128]{3,2,1,0:T(8,128)(2,1)S(1)}, u32[]{:S(2)}, u32[]{:S(2)}) collective-permute-start(bf16[1,8,64,128]{3,2,1,0:T(8,128)(2,1)S(1)} %get-tuple-element.38), channel_id=1, source_target_pairs={{0,8},{8,0},{16,24},{24,16},{32,40},{40,32},{48,56},{56,48},{64,72... | collective-permute-start | bytes 393224 | tf_op jit(solution)/shard_map/ppermute | solution.py:50
  76.8 3.8 %copy-start.14 = (bf16[6,4,8,64,128]{4,3,2,1,0:T(8,128)(2,1)S(1)}, bf16[6,4,8,64,128]{4,3,2,1,0:T(8,128)(2,1)}, u32[]{:S(2)}) copy-start(bf16[6,4,8,64,128]{4,3,2,1,0:T(8,128)(2,1)} %copy-done.13) | copy-start | bytes 9437188
  76.9 3.8 %copy-start.26 = (f32[6,4,8,64]{3,2,1,0:T(8,128)S(1)}, f32[6,4,8,64]{3,2,1,0:T(8,128)}, u32[]{:S(2)}) copy-start(f32[6,4,8,64]{3,2,1,0:T(8,128)} %broadcast_divide_fusion.1) | copy-start | bytes 147460
  86.3 5.5 %copy-start.1 = (bf16[6,4,8,64,128]{4,3,2,1,0:T(8,128)(2,1)S(1)}, bf16[6,4,8,64,128]{4,3,2,1,0:T(8,128)(2,1)}, u32[]{:S(2)}) copy-start(bf16[6,4,8,64,128]{4,3,2,1,0:T(8,128)(2,1)} %param.8) | copy-start | bytes 9437188
  93.0 1.9 %copy-start.9 = (f32[4,8,64,128]{3,2,1,0:T(8,128)}, f32[4,8,64,128]{3,2,1,0:T(8,128)S(1)}, u32[]{:S(2)}) copy-start(f32[4,8,64,128]{3,2,1,0:T(8,128)S(1)} %get-tuple-element.5) | copy-start | bytes 3145732
  93.0 1.9 %copy-start.5 = (f32[4,8,64,128]{3,2,1,0:T(8,128)}, f32[4,8,64,128]{3,2,1,0:T(8,128)S(1)}, u32[]{:S(2)}) copy-start(f32[4,8,64,128]{3,2,1,0:T(8,128)S(1)} %get-tuple-element.7) | copy-start | bytes 3145732
  93.5 1.5 copy-start.6
  93.5 11.3 %collective-permute-start.14 = (bf16[4,8,1,128]{3,2,1,0:T(2,128)(2,1)S(1)}, bf16[4,8,1,128]{3,2,1,0:T(2,128)(2,1)S(1)}, u32[]{:S(2)}, u32[]{:S(2)}) collective-permute-start(bf16[4,8,1,128]{3,2,1,0:T(2,128)(2,1)S(1)} %broadcast_select_fusion.21), channel_id=1, source_target_pairs={{0,1},{1,0},{2,3},{3,2},{4,5},{5,4},{6,7},{7,6},{8,9},{9,8},{10,11... | collective-permute-start | bytes 24584 | tf_op jit(solution)/shard_map/ppermute | solution.py:50
  94.9 1.3 copy-start.21
  94.9 13.1 %slice-start.2 = ((s8[6291456]{0:T(1024)(128)(4,1)}), s8[2097152]{0:T(1024)(128)(4,1)S(1)}, s32[]{:S(2)}) async-start(s8[6291456]{0:T(1024)(128)(4,1)} %bitcast.364), calls=%async_computation.4 | async-start | bytes 4194304
  96.2 11.9 %slice-start.3 = ((s8[6291456]{0:T(1024)(128)(4,1)}), s8[4194304]{0:T(1024)(128)(4,1)S(1)}, s32[]{:S(2)}) async-start(s8[6291456]{0:T(1024)(128)(4,1)} %bitcast.364), calls=%async_computation.5 | async-start | bytes 8388608
  96.2 11.2 %slice-start.4 = ((bf16[4,8,64,128]{3,2,1,0:T(8,128)(2,1)}), bf16[3,8,64,128]{3,2,1,0:T(8,128)(2,1)S(1)}, s32[]{:S(2)}) async-start(bf16[4,8,64,128]{3,2,1,0:T(8,128)(2,1)} %copy-done.21), calls=%async_computation.6 | async-start | bytes 786432 | tf_op jit(solution)/shard_map/slice | solution.py:106
  96.5 8.4 %collective-permute-start.12 = (bf16[4,1,64,128]{3,2,1,0:T(8,128)(2,1)S(1)}, bf16[4,1,64,128]{3,2,1,0:T(8,128)(2,1)S(1)}, u32[]{:S(2)}, u32[]{:S(2)}) collective-permute-start(bf16[4,1,64,128]{3,2,1,0:T(8,128)(2,1)S(1)} %get-tuple-element.28), channel_id=1, source_target_pairs={{2,4},{4,2},{3,5},{5,3},{10,12},{12,10},{11,13},{13,11},{18,20},{2... | collective-permute-start | bytes 196616 | tf_op jit(solution)/shard_map/ppermute | solution.py:54
  97.3 7.6 %collective-permute-start.13 = (bf16[4,1,64,128]{3,2,1,0:T(8,128)(2,1)S(1)}, bf16[4,1,64,128]{3,2,1,0:T(8,128)(2,1)S(1)}, u32[]{:S(2)}, u32[]{:S(2)}) collective-permute-start(bf16[4,1,64,128]{3,2,1,0:T(8,128)(2,1)S(1)} %get-tuple-element.27), channel_id=1, source_target_pairs={{0,2},{2,0},{4,6},{6,4},{1,3},{3,1},{5,7},{7,5},{8,10},{10,8},{12,... | collective-permute-start | bytes 196616 | tf_op jit(solution)/shard_map/ppermute | solution.py:50
  100.3 7.1 %collective-permute-start.10 = (bf16[1,8,64,128]{3,2,1,0:T(8,128)(2,1)S(1)}, bf16[1,8,64,128]{3,2,1,0:T(8,128)(2,1)S(1)}, u32[]{:S(2)}, u32[]{:S(2)}) collective-permute-start(bf16[1,8,64,128]{3,2,1,0:T(8,128)(2,1)S(1)} %get-tuple-element.30), channel_id=1, source_target_pairs={{8,16},{16,8},{24,32},{32,24},{40,48},{48,40},{56,64},{64,56},{72,... | collective-permute-start | bytes 393224 | tf_op jit(solution)/shard_map/ppermute | solution.py:54
  104.7 2.6 %collective-permute-start.11 = (bf16[1,8,64,128]{3,2,1,0:T(8,128)(2,1)S(1)}, bf16[1,8,64,128]{3,2,1,0:T(8,128)(2,1)S(1)}, u32[]{:S(2)}, u32[]{:S(2)}) collective-permute-start(bf16[1,8,64,128]{3,2,1,0:T(8,128)(2,1)S(1)} %get-tuple-element.29), channel_id=1, source_target_pairs={{0,8},{8,0},{16,24},{24,16},{32,40},{40,32},{48,56},{56,48},{64,72... | collective-permute-start | bytes 393224 | tf_op jit(solution)/shard_map/ppermute | solution.py:50
  108.0 3.9 %copy-start.7 = (bf16[6,4,8,64,128]{4,3,2,1,0:T(8,128)(2,1)}, bf16[6,4,8,64,128]{4,3,2,1,0:T(8,128)(2,1)S(1)}, u32[]{:S(2)}) copy-start(bf16[6,4,8,64,128]{4,3,2,1,0:T(8,128)(2,1)S(1)} %fusion.66) | copy-start | bytes 9437188
  108.1 3.9 %copy-start.12 = (bf16[6,4,8,64,128]{4,3,2,1,0:T(8,128)(2,1)S(1)}, bf16[6,4,8,64,128]{4,3,2,1,0:T(8,128)(2,1)}, u32[]{:S(2)}) copy-start(bf16[6,4,8,64,128]{4,3,2,1,0:T(8,128)(2,1)} %copy-done.11) | copy-start | bytes 9437188
  108.1 3.9 %copy-start.25 = (f32[6,4,8,64]{3,2,1,0:T(8,128)S(1)}, f32[6,4,8,64]{3,2,1,0:T(8,128)}, u32[]{:S(2)}) copy-start(f32[6,4,8,64]{3,2,1,0:T(8,128)} %broadcast_divide_fusion) | copy-start | bytes 147460
  112.0 28.1 %copy-start.24 = (f32[6,128,128]{2,1,0:T(8,128)S(1)}, f32[6,128,128]{2,1,0:T(8,128)}, u32[]{:S(2)}) copy-start(f32[6,128,128]{2,1,0:T(8,128)} %get-tuple-element.44) | copy-start | bytes 1179652
  118.2 39.2 %all-to-all-start = ((f32[256,1,384]{2,1,0:T(1,128)}), f32[256,1,384]{2,1,0:T(1,128)}, u32[]{:S(2)}, u32[]{:S(2)}) async-start(f32[256,1,384]{2,1,0:T(1,128)} %bitcast.75), calls=%async_computation | async-start | bytes 786432 | tf_op jit(solution)/shard_map/all_to_all | solution.py:166
  140.9 25.3 %copy-start.2 = (bf16[6,4,8,64,128]{4,3,2,1,0:T(8,128)(2,1)S(1)}, bf16[6,4,8,64,128]{4,3,2,1,0:T(8,128)(2,1)}, u32[]{:S(2)}) copy-start(bf16[6,4,8,64,128]{4,3,2,1,0:T(8,128)(2,1)} %param.8) | copy-start | bytes 9437188
  160.4 24.2 %all-to-all-start.1 = ((f32[256,1,384]{2,1,0:T(1,128)}), f32[256,1,384]{2,1,0:T(1,128)S(1)}, u32[]{:S(2)}, u32[]{:S(2)}) async-start(f32[256,1,384]{2,1,0:T(1,128)} %broadcast_in_dim.27), calls=%async_computation.1 | async-start | bytes 786432 | tf_op jit(solution)/shard_map/all_to_all | solution.py:169
